TPU v7x, 32 devices: a whole 2x2x4 slice. The times are simulated.
32 devices in a mesh: row: 4 (over z), col: 4 (over y, x), batch: 2 (over core).
Axes of the slice: x: 2, y: 2, z: 4, core: 2. Of those that a mesh axis runs over, the one named last changes fastest.
Arguments:
- green: bfloat16 [4, 4, 2048, 2048], P('row', 'col'), may hold values from -0.125 to 0.125
- background: bfloat16 [4, 4, 512, 2048], P('row', 'col', 'batch'), parts along dimension 2, may hold values from -3 to 3
- wavelet: bfloat16 [512, 2048], P('batch'), parts along dimension 0, may hold values from -6 to 6
- station_cell: int32 [512], P('batch'), parts along dimension 0, may hold values from 0 to 15
- fault_point: int32 [4, 64], P('row', 'col'), may hold values from 0 to 2047
- fault_owner: int32 [4, 64, 1], P('row', 'col'), may hold values from 0 to 3; in each aligned block of 16 rows (0 to 15, 16 to 31, ..., all dimensions but the last counted through in order) at most 8 rows name the same one
- fault_row: int32 [4, 64], P('row', 'col'), may hold values from 0 to 127
Outputs:
- sweep: bfloat16 [4, 4, 512, 2048], P('row', 'col', 'batch'), parts along dimension 2
- database: float32 [4, 4, 128, 512], P('row', 'col', None, 'batch'), parts along dimension 3
There are 2 independent parts, one for each index of `batch`. A program takes and returns all parts, laid end to end along the dimension named above; an argument that names none is the same for every part. Nothing has to cross between parts.
Inputs may be any that keep to these rules, and one draw needn't show every extreme that they name: `fault_owner`: among the 16 fault points of one subdomain no owner is named more than 8 times, and in every draw some subdomain names some owner exactly 8 times.
All inputs are finite; a program needn't handle non-finite values.
Results may differ from a plain program's by a relative error of at most 0.02.
Values may be sent and summed in bfloat16 or wider, within the bound.
No kernel may reach another device: no remote copies, remote signals or barrier semaphores. Data moves between devices by JAX's collectives and lax.ppermute only.
A program may use at most 64 MiB of HBM per device.

v0:
```python
import jax
import jax.numpy as jnp
from jax import lax
from jax.sharding import PartitionSpec as P

DB = 128


def passed_along(shard, axis, by):
    peers = lax.axis_size(axis)
    pairs = [(i, i + by) for i in range(peers) if 0 <= i + by < peers]
    return lax.ppermute(shard, axis, pairs)


def on_device(green, background, wavelet, station_cell, fault_point, fault_owner, fault_row):
    row_place = lax.axis_index("row")
    col_place = lax.axis_index("col")
    row_count = lax.axis_size("row")
    col_count = lax.axis_size("col")
    matrix = green[0, 0]
    half = matrix.shape[0] // 2
    stations = background.shape[2]
    wave_float = wavelet.astype(jnp.float32)
    own_source = (station_cell == row_place * col_count + col_place)[:, None]
    source = background[0, 0].astype(jnp.float32) + jnp.where(
        own_source, wave_float, jnp.zeros_like(wave_float)
    )
    blocks = 2
    height = stations // blocks
    total_fronts = row_count + col_count + blocks - 2

    def advance(moment, carry):
        down_in, right_in, field = carry
        block = moment - row_place - col_place
        active = jnp.logical_and(block >= 0, block < blocks)
        start = jnp.clip(block, 0, blocks - 1) * height
        joined = jnp.concatenate([down_in, right_in], axis=1)
        update = jnp.dot(
            joined, matrix, preferred_element_type=jnp.float32
        ) + lax.dynamic_slice_in_dim(source, start, height, 0)
        update = jnp.where(active, update, jnp.zeros_like(update)).astype(jnp.bfloat16)
        previous = lax.dynamic_slice_in_dim(field, start, height, 0)
        field = lax.dynamic_update_slice_in_dim(
            field, jnp.where(active, update, previous), start, 0
        )
        down_next = passed_along(update[:, :half], "row", 1)
        right_next = passed_along(update[:, half:], "col", 1)
        return (down_next, right_next, field)

    empty_face = jnp.zeros((height, half), jnp.bfloat16)
    empty_field = jnp.zeros((stations, 2 * half), jnp.bfloat16)
    finished = lax.fori_loop(0, total_fronts, advance, (empty_face, empty_face, empty_field))
    field = finished[2]
    points = fault_point[0]
    owners = fault_owner[0, :, 0]
    targets = fault_row[0]
    listed = points.shape[0]
    point_hot = (points[:, None] == jnp.arange(2 * half, dtype=jnp.int32)[None, :]).astype(
        jnp.bfloat16
    )
    traces = jnp.einsum("qp,sp->qs", point_hot, field, preferred_element_type=jnp.float32).astype(
        jnp.bfloat16
    )
    capacity = 2 * listed // col_count
    owner_hot = (owners[:, None] == jnp.arange(col_count, dtype=jnp.int32)[None, :]).astype(
        jnp.int32
    )
    running = jnp.cumsum(owner_hot, axis=0) - 1
    rank = jnp.sum(owner_hot * running, axis=1)
    slots = owners * capacity + rank
    slot_match = slots[None, :] == jnp.arange(col_count * capacity, dtype=jnp.int32)[:, None]
    slot_hot = slot_match.astype(jnp.bfloat16)
    packed = jnp.dot(slot_hot, traces, preferred_element_type=jnp.float32).astype(jnp.bfloat16)
    packed = packed.reshape(col_count, capacity, stations)
    slot_rows = jnp.sum(jnp.where(slot_match, targets[None, :] + 1, 0), axis=1) - 1
    slot_rows = slot_rows.astype(jnp.float32).astype(jnp.bfloat16).reshape(col_count, capacity)
    arrived, arrived_rows = (
        lax.all_to_all(packed, "col", split_axis=0, concat_axis=0, tiled=True),
        lax.all_to_all(slot_rows, "col", split_axis=0, concat_axis=0, tiled=True),
    )
    row_numbers = arrived_rows.reshape(-1).astype(jnp.int32)
    table_hot = (row_numbers[None, :] == jnp.arange(DB, dtype=jnp.int32)[:, None]).astype(
        jnp.bfloat16
    )
    database = jnp.dot(
        table_hot,
        arrived.reshape(col_count * capacity, stations),
        preferred_element_type=jnp.float32,
    )
    return (field[None, None], database[None, None])


def solution(mesh):
    in_specs = (
        P("row", "col", None, None),
        P("row", "col", "batch", None),
        P("batch", None),
        P("batch"),
        P("row", "col"),
        P("row", "col", None),
        P("row", "col"),
    )
    out_specs = (P("row", "col", "batch", None), P("row", "col", None, "batch"))
    return jax.shard_map(
        on_device, mesh=mesh, in_specs=in_specs, out_specs=out_specs, check_vma=False
    )
```

profile of v0, /device:TPU:0, one launch (start us, length us, event | category | flops | bytes accessed | tf_op | source)
XLA Modules:
  0.0 165.4 jit_solution(13230295084055159790)
XLA Ops:
  4.3 5.2 %all-to-all-start = ((bf16[4,1,8]{2,1,0:T(2,128)(2,1)}), bf16[4,1,8]{2,1,0:T(2,128)(2,1)S(1)}, u32[]{:S(2)}, u32[]{:S(2)}) async-start(bf16[4,1,8]{2,1,0:T(2,128)(2,1)} %convert_element_type.77), calls=%async_computation | async-start | bytes 4096 | tf_op jit(solution)/shard_map/all_to_all | solution.py:79
  12.9 139.3 %while.17 = (s32[]{:T(128)}, bf16[128,1024]{1,0:T(8,128)(2,1)S(1)}, bf16[128,1024]{1,0:T(8,128)(2,1)}, bf16[256,2048]{1,0:T(8,128)(2,1)S(1)}, s32[]{:T(128)}, /*...) while((s32[]{:T(128)}, bf16[128,1024]{1,0:T(8,128)(2,1)S(1)}, ...), condition=%wide.region_1.2_spmd, body=%wide.region_0.1_spmd.sunk | while | flops 1075838976 | bytes 14680389 | solution.py:52
  12.9 4.9 %select_dynamic-update-slice_fusion.2 = (bf16[256,2048]{1,0:T(8,128)(2,1)S(1)}, bf16[128,2048]{1,0:T(8,128)(2,1)S(1)}) fusion(bf16[256,2048]{1,0:T(8,128)(2,1)S(1)} %get-tuple-element.235, s32[]{:T(128)S(6)} %select_n.58, pred[]{:T(512)S(6)} %and.10, f32[256,2048]{1,0:T(8,128)S(1)} %get-tuple-element.252, bf16[2048,2048]{1,0:T(8,128)(2,1)} %get-tuple-element.251, ...), kind=kOutput, calls=%fused_computation.6.clone.1 | convolution fusion | flops 1075838976 | bytes 11534341 | tf_op jit(solution)/shard_map/while/body/eval_jaxpr/dot_general | solution.py:38
  18.7 3.5 %collective-permute-start = (bf16[128,1024]{1,0:T(8,128)(2,1)}, bf16[128,1024]{1,0:T(8,128)(2,1)S(1)}, u32[]{:S(2)}, u32[]{:S(2)}) collective-permute-start(bf16[128,1024]{1,0:T(8,128)(2,1)} %get-tuple-element.216), channel_id=1, source_target_pairs={{0,8},{8,16},{16,24},{1,9},{9,17},{17,25},{2,10},{10,18},{18,26},{... | collective-permute-start | bytes 786440 | tf_op jit(solution)/shard_map/while/body/eval_jaxpr/ppermute | solution.py:12
  22.2 4.6 %collective-permute-start.1 = (bf16[128,1024]{1,0:T(8,128)(2,1)}, bf16[128,1024]{1,0:T(8,128)(2,1)}, u32[]{:S(2)}, u32[]{:S(2)}) collective-permute-start(bf16[128,1024]{1,0:T(8,128)(2,1)} %get-tuple-element.217), channel_id=1, source_target_pairs={{0,2},{2,4},{4,6},{1,3},{3,5},{5,7},{8,10},{10,12},{12,14},{9,11},... | collective-permute-start | bytes 786440 | tf_op jit(solution)/shard_map/while/body/eval_jaxpr/ppermute | solution.py:12
  27.7 3.4 %collective-permute-done.1 = bf16[128,1024]{1,0:T(8,128)(2,1)} collective-permute-done((bf16[128,1024]{1,0:T(8,128)(2,1)}, bf16[128,1024]{1,0:T(8,128)(2,1)}, u32[]{:S(2)}, u32[]{:S(2)}) %collective-permute-start.1) | collective-permute-done | bytes 262176 | tf_op jit(solution)/shard_map/while/body/eval_jaxpr/ppermute | solution.py:12
  31.1 4.9 %select_dynamic-update-slice_fusion.2 = (bf16[256,2048]{1,0:T(8,128)(2,1)S(1)}, bf16[128,2048]{1,0:T(8,128)(2,1)S(1)}) fusion(bf16[256,2048]{1,0:T(8,128)(2,1)S(1)} %get-tuple-element.235, s32[]{:T(128)S(6)} %select_n.58, pred[]{:T(512)S(6)} %and.10, f32[256,2048]{1,0:T(8,128)S(1)} %get-tuple-element.252, bf16[2048,2048]{1,0:T(8,128)(2,1)} %get-tuple-element.251, ...), kind=kOutput, calls=%fused_computation.6.clone.1 | convolution fusion | flops 1075838976 | bytes 11534341 | tf_op jit(solution)/shard_map/while/body/eval_jaxpr/dot_general | solution.py:38
  36.8 3.5 %collective-permute-start = (bf16[128,1024]{1,0:T(8,128)(2,1)}, bf16[128,1024]{1,0:T(8,128)(2,1)S(1)}, u32[]{:S(2)}, u32[]{:S(2)}) collective-permute-start(bf16[128,1024]{1,0:T(8,128)(2,1)} %get-tuple-element.216), channel_id=1, source_target_pairs={{0,8},{8,16},{16,24},{1,9},{9,17},{17,25},{2,10},{10,18},{18,26},{... | collective-permute-start | bytes 786440 | tf_op jit(solution)/shard_map/while/body/eval_jaxpr/ppermute | solution.py:12
  40.3 5.1 %collective-permute-start.1 = (bf16[128,1024]{1,0:T(8,128)(2,1)}, bf16[128,1024]{1,0:T(8,128)(2,1)}, u32[]{:S(2)}, u32[]{:S(2)}) collective-permute-start(bf16[128,1024]{1,0:T(8,128)(2,1)} %get-tuple-element.217), channel_id=1, source_target_pairs={{0,2},{2,4},{4,6},{1,3},{3,5},{5,7},{8,10},{10,12},{12,14},{9,11},... | collective-permute-start | bytes 786440 | tf_op jit(solution)/shard_map/while/body/eval_jaxpr/ppermute | solution.py:12
  45.4 3.5 %collective-permute-done.1 = bf16[128,1024]{1,0:T(8,128)(2,1)} collective-permute-done((bf16[128,1024]{1,0:T(8,128)(2,1)}, bf16[128,1024]{1,0:T(8,128)(2,1)}, u32[]{:S(2)}, u32[]{:S(2)}) %collective-permute-start.1) | collective-permute-done | bytes 262176 | tf_op jit(solution)/shard_map/while/body/eval_jaxpr/ppermute | solution.py:12
  48.9 4.9 %select_dynamic-update-slice_fusion.2 = (bf16[256,2048]{1,0:T(8,128)(2,1)S(1)}, bf16[128,2048]{1,0:T(8,128)(2,1)S(1)}) fusion(bf16[256,2048]{1,0:T(8,128)(2,1)S(1)} %get-tuple-element.235, s32[]{:T(128)S(6)} %select_n.58, pred[]{:T(512)S(6)} %and.10, f32[256,2048]{1,0:T(8,128)S(1)} %get-tuple-element.252, bf16[2048,2048]{1,0:T(8,128)(2,1)} %get-tuple-element.251, ...), kind=kOutput, calls=%fused_computation.6.clone.1 | convolution fusion | flops 1075838976 | bytes 11534341 | tf_op jit(solution)/shard_map/while/body/eval_jaxpr/dot_general | solution.py:38
  54.6 3.5 %collective-permute-start = (bf16[128,1024]{1,0:T(8,128)(2,1)}, bf16[128,1024]{1,0:T(8,128)(2,1)S(1)}, u32[]{:S(2)}, u32[]{:S(2)}) collective-permute-start(bf16[128,1024]{1,0:T(8,128)(2,1)} %get-tuple-element.216), channel_id=1, source_target_pairs={{0,8},{8,16},{16,24},{1,9},{9,17},{17,25},{2,10},{10,18},{18,26},{... | collective-permute-start | bytes 786440 | tf_op jit(solution)/shard_map/while/body/eval_jaxpr/ppermute | solution.py:12
  58.1 5.1 %collective-permute-start.1 = (bf16[128,1024]{1,0:T(8,128)(2,1)}, bf16[128,1024]{1,0:T(8,128)(2,1)}, u32[]{:S(2)}, u32[]{:S(2)}) collective-permute-start(bf16[128,1024]{1,0:T(8,128)(2,1)} %get-tuple-element.217), channel_id=1, source_target_pairs={{0,2},{2,4},{4,6},{1,3},{3,5},{5,7},{8,10},{10,12},{12,14},{9,11},... | collective-permute-start | bytes 786440 | tf_op jit(solution)/shard_map/while/body/eval_jaxpr/ppermute | solution.py:12
  63.2 3.5 %collective-permute-done.1 = bf16[128,1024]{1,0:T(8,128)(2,1)} collective-permute-done((bf16[128,1024]{1,0:T(8,128)(2,1)}, bf16[128,1024]{1,0:T(8,128)(2,1)}, u32[]{:S(2)}, u32[]{:S(2)}) %collective-permute-start.1) | collective-permute-done | bytes 262176 | tf_op jit(solution)/shard_map/while/body/eval_jaxpr/ppermute | solution.py:12
  66.7 4.9 %select_dynamic-update-slice_fusion.2 = (bf16[256,2048]{1,0:T(8,128)(2,1)S(1)}, bf16[128,2048]{1,0:T(8,128)(2,1)S(1)}) fusion(bf16[256,2048]{1,0:T(8,128)(2,1)S(1)} %get-tuple-element.235, s32[]{:T(128)S(6)} %select_n.58, pred[]{:T(512)S(6)} %and.10, f32[256,2048]{1,0:T(8,128)S(1)} %get-tuple-element.252, bf16[2048,2048]{1,0:T(8,128)(2,1)} %get-tuple-element.251, ...), kind=kOutput, calls=%fused_computation.6.clone.1 | convolution fusion | flops 1075838976 | bytes 11534341 | tf_op jit(solution)/shard_map/while/body/eval_jaxpr/dot_general | solution.py:38
  72.4 1.9 %collective-permute-start = (bf16[128,1024]{1,0:T(8,128)(2,1)}, bf16[128,1024]{1,0:T(8,128)(2,1)S(1)}, u32[]{:S(2)}, u32[]{:S(2)}) collective-permute-start(bf16[128,1024]{1,0:T(8,128)(2,1)} %get-tuple-element.216), channel_id=1, source_target_pairs={{0,8},{8,16},{16,24},{1,9},{9,17},{17,25},{2,10},{10,18},{18,26},{... | collective-permute-start | bytes 786440 | tf_op jit(solution)/shard_map/while/body/eval_jaxpr/ppermute | solution.py:12
  74.3 5.9 %collective-permute-start.1 = (bf16[128,1024]{1,0:T(8,128)(2,1)}, bf16[128,1024]{1,0:T(8,128)(2,1)}, u32[]{:S(2)}, u32[]{:S(2)}) collective-permute-start(bf16[128,1024]{1,0:T(8,128)(2,1)} %get-tuple-element.217), channel_id=1, source_target_pairs={{0,2},{2,4},{4,6},{1,3},{3,5},{5,7},{8,10},{10,12},{12,14},{9,11},... | collective-permute-start | bytes 786440 | tf_op jit(solution)/shard_map/while/body/eval_jaxpr/ppermute | solution.py:12
  80.2 3.5 %collective-permute-done.1 = bf16[128,1024]{1,0:T(8,128)(2,1)} collective-permute-done((bf16[128,1024]{1,0:T(8,128)(2,1)}, bf16[128,1024]{1,0:T(8,128)(2,1)}, u32[]{:S(2)}, u32[]{:S(2)}) %collective-permute-start.1) | collective-permute-done | bytes 262176 | tf_op jit(solution)/shard_map/while/body/eval_jaxpr/ppermute | solution.py:12
  83.7 4.9 %select_dynamic-update-slice_fusion.2 = (bf16[256,2048]{1,0:T(8,128)(2,1)S(1)}, bf16[128,2048]{1,0:T(8,128)(2,1)S(1)}) fusion(bf16[256,2048]{1,0:T(8,128)(2,1)S(1)} %get-tuple-element.235, s32[]{:T(128)S(6)} %select_n.58, pred[]{:T(512)S(6)} %and.10, f32[256,2048]{1,0:T(8,128)S(1)} %get-tuple-element.252, bf16[2048,2048]{1,0:T(8,128)(2,1)} %get-tuple-element.251, ...), kind=kOutput, calls=%fused_computation.6.clone.1 | convolution fusion | flops 1075838976 | bytes 11534341 | tf_op jit(solution)/shard_map/while/body/eval_jaxpr/dot_general | solution.py:38
  91.3 6.0 %collective-permute-start.1 = (bf16[128,1024]{1,0:T(8,128)(2,1)}, bf16[128,1024]{1,0:T(8,128)(2,1)}, u32[]{:S(2)}, u32[]{:S(2)}) collective-permute-start(bf16[128,1024]{1,0:T(8,128)(2,1)} %get-tuple-element.217), channel_id=1, source_target_pairs={{0,2},{2,4},{4,6},{1,3},{3,5},{5,7},{8,10},{10,12},{12,14},{9,11},... | collective-permute-start | bytes 786440 | tf_op jit(solution)/shard_map/while/body/eval_jaxpr/ppermute | solution.py:12
  97.3 3.5 %collective-permute-done.1 = bf16[128,1024]{1,0:T(8,128)(2,1)} collective-permute-done((bf16[128,1024]{1,0:T(8,128)(2,1)}, bf16[128,1024]{1,0:T(8,128)(2,1)}, u32[]{:S(2)}, u32[]{:S(2)}) %collective-permute-start.1) | collective-permute-done | bytes 262176 | tf_op jit(solution)/shard_map/while/body/eval_jaxpr/ppermute | solution.py:12
  100.8 4.9 %select_dynamic-update-slice_fusion.2 = (bf16[256,2048]{1,0:T(8,128)(2,1)S(1)}, bf16[128,2048]{1,0:T(8,128)(2,1)S(1)}) fusion(bf16[256,2048]{1,0:T(8,128)(2,1)S(1)} %get-tuple-element.235, s32[]{:T(128)S(6)} %select_n.58, pred[]{:T(512)S(6)} %and.10, f32[256,2048]{1,0:T(8,128)S(1)} %get-tuple-element.252, bf16[2048,2048]{1,0:T(8,128)(2,1)} %get-tuple-element.251, ...), kind=kOutput, calls=%fused_computation.6.clone.1 | convolution fusion | flops 1075838976 | bytes 11534341 | tf_op jit(solution)/shard_map/while/body/eval_jaxpr/dot_general | solution.py:38
  108.5 6.0 %collective-permute-start.1 = (bf16[128,1024]{1,0:T(8,128)(2,1)}, bf16[128,1024]{1,0:T(8,128)(2,1)}, u32[]{:S(2)}, u32[]{:S(2)}) collective-permute-start(bf16[128,1024]{1,0:T(8,128)(2,1)} %get-tuple-element.217), channel_id=1, source_target_pairs={{0,2},{2,4},{4,6},{1,3},{3,5},{5,7},{8,10},{10,12},{12,14},{9,11},... | collective-permute-start | bytes 786440 | tf_op jit(solution)/shard_map/while/body/eval_jaxpr/ppermute | solution.py:12
  114.5 3.5 %collective-permute-done.1 = bf16[128,1024]{1,0:T(8,128)(2,1)} collective-permute-done((bf16[128,1024]{1,0:T(8,128)(2,1)}, bf16[128,1024]{1,0:T(8,128)(2,1)}, u32[]{:S(2)}, u32[]{:S(2)}) %collective-permute-start.1) | collective-permute-done | bytes 262176 | tf_op jit(solution)/shard_map/while/body/eval_jaxpr/ppermute | solution.py:12
  117.9 4.9 %select_dynamic-update-slice_fusion.2 = (bf16[256,2048]{1,0:T(8,128)(2,1)S(1)}, bf16[128,2048]{1,0:T(8,128)(2,1)S(1)}) fusion(bf16[256,2048]{1,0:T(8,128)(2,1)S(1)} %get-tuple-element.235, s32[]{:T(128)S(6)} %select_n.58, pred[]{:T(512)S(6)} %and.10, f32[256,2048]{1,0:T(8,128)S(1)} %get-tuple-element.252, bf16[2048,2048]{1,0:T(8,128)(2,1)} %get-tuple-element.251, ...), kind=kOutput, calls=%fused_computation.6.clone.1 | convolution fusion | flops 1075838976 | bytes 11534341 | tf_op jit(solution)/shard_map/while/body/eval_jaxpr/dot_general | solution.py:38
  125.6 6.0 %collective-permute-start.1 = (bf16[128,1024]{1,0:T(8,128)(2,1)}, bf16[128,1024]{1,0:T(8,128)(2,1)}, u32[]{:S(2)}, u32[]{:S(2)}) collective-permute-start(bf16[128,1024]{1,0:T(8,128)(2,1)} %get-tuple-element.217), channel_id=1, source_target_pairs={{0,2},{2,4},{4,6},{1,3},{3,5},{5,7},{8,10},{10,12},{12,14},{9,11},... | collective-permute-start | bytes 786440 | tf_op jit(solution)/shard_map/while/body/eval_jaxpr/ppermute | solution.py:12
  131.6 3.5 %collective-permute-done.1 = bf16[128,1024]{1,0:T(8,128)(2,1)} collective-permute-done((bf16[128,1024]{1,0:T(8,128)(2,1)}, bf16[128,1024]{1,0:T(8,128)(2,1)}, u32[]{:S(2)}, u32[]{:S(2)}) %collective-permute-start.1) | collective-permute-done | bytes 262176 | tf_op jit(solution)/shard_map/while/body/eval_jaxpr/ppermute | solution.py:12
  135.1 4.9 %select_dynamic-update-slice_fusion.2 = (bf16[256,2048]{1,0:T(8,128)(2,1)S(1)}, bf16[128,2048]{1,0:T(8,128)(2,1)S(1)}) fusion(bf16[256,2048]{1,0:T(8,128)(2,1)S(1)} %get-tuple-element.235, s32[]{:T(128)S(6)} %select_n.58, pred[]{:T(512)S(6)} %and.10, f32[256,2048]{1,0:T(8,128)S(1)} %get-tuple-element.252, bf16[2048,2048]{1,0:T(8,128)(2,1)} %get-tuple-element.251, ...), kind=kOutput, calls=%fused_computation.6.clone.1 | convolution fusion | flops 1075838976 | bytes 11534341 | tf_op jit(solution)/shard_map/while/body/eval_jaxpr/dot_general | solution.py:38
  142.7 6.0 %collective-permute-start.1 = (bf16[128,1024]{1,0:T(8,128)(2,1)}, bf16[128,1024]{1,0:T(8,128)(2,1)}, u32[]{:S(2)}, u32[]{:S(2)}) collective-permute-start(bf16[128,1024]{1,0:T(8,128)(2,1)} %get-tuple-element.217), channel_id=1, source_target_pairs={{0,2},{2,4},{4,6},{1,3},{3,5},{5,7},{8,10},{10,12},{12,14},{9,11},... | collective-permute-start | bytes 786440 | tf_op jit(solution)/shard_map/while/body/eval_jaxpr/ppermute | solution.py:12
  148.7 3.6 %collective-permute-done.1 = bf16[128,1024]{1,0:T(8,128)(2,1)} collective-permute-done((bf16[128,1024]{1,0:T(8,128)(2,1)}, bf16[128,1024]{1,0:T(8,128)(2,1)}, u32[]{:S(2)}, u32[]{:S(2)}) %collective-permute-start.1) | collective-permute-done | bytes 262176 | tf_op jit(solution)/shard_map/while/body/eval_jaxpr/ppermute | solution.py:12
  153.4 6.5 %all-to-all-start.1 = ((bf16[4,8,256]{2,1,0:T(8,128)(2,1)}), bf16[4,8,256]{2,1,0:T(8,128)(2,1)S(1)}, u32[]{:S(2)}, u32[]{:S(2)}) async-start(bf16[4,8,256]{2,1,0:T(8,128)(2,1)} %fusion.6), calls=%async_computation.1 | async-start | bytes 32768 | tf_op jit(solution)/shard_map/all_to_all | solution.py:78
  160.0 4.6 %all-to-all-done.1 = bf16[4,8,256]{2,1,0:T(8,128)(2,1)S(1)} async-done(((bf16[4,8,256]{2,1,0:T(8,128)(2,1)}), bf16[4,8,256]{2,1,0:T(8,128)(2,1)S(1)}, u32[]{:S(2)}, u32[]{:S(2)}) %all-to-all-start.1) | async-done | bytes 16416 | tf_op jit(solution)/shard_map/all_to_all | solution.py:78
  (42 shorter events, 24.3 us)
Async XLA Ops:
  4.3 149.1 %all-to-all-start = ((bf16[4,1,8]{2,1,0:T(2,128)(2,1)}), bf16[4,1,8]{2,1,0:T(2,128)(2,1)S(1)}, u32[]{:S(2)}, u32[]{:S(2)}) async-start(bf16[4,1,8]{2,1,0:T(2,128)(2,1)} %convert_element_type.77), calls=%async_computation | async-start | bytes 4096 | tf_op jit(solution)/shard_map/all_to_all | solution.py:79
  12.9 139.3 %copy-start.1 = (s32[1,16]{1,0:T(1,128)S(1)}, s32[1,16]{1,0:T(1,128)}, u32[]{:S(2)}) copy-start(s32[1,16]{1,0:T(1,128)} %param.13) | copy-start | bytes 196
  18.7 9.1 %collective-permute-start = (bf16[128,1024]{1,0:T(8,128)(2,1)}, bf16[128,1024]{1,0:T(8,128)(2,1)S(1)}, u32[]{:S(2)}, u32[]{:S(2)}) collective-permute-start(bf16[128,1024]{1,0:T(8,128)(2,1)} %get-tuple-element.216), channel_id=1, source_target_pairs={{0,8},{8,16},{16,24},{1,9},{9,17},{17,25},{2,10},{10,18},{18,26},{... | collective-permute-start | bytes 786440 | tf_op jit(solution)/shard_map/while/body/eval_jaxpr/ppermute | solution.py:12
  22.2 9.0 %collective-permute-start.1 = (bf16[128,1024]{1,0:T(8,128)(2,1)}, bf16[128,1024]{1,0:T(8,128)(2,1)}, u32[]{:S(2)}, u32[]{:S(2)}) collective-permute-start(bf16[128,1024]{1,0:T(8,128)(2,1)} %get-tuple-element.217), channel_id=1, source_target_pairs={{0,2},{2,4},{4,6},{1,3},{3,5},{5,7},{8,10},{10,12},{12,14},{9,11},... | collective-permute-start | bytes 786440 | tf_op jit(solution)/shard_map/while/body/eval_jaxpr/ppermute | solution.py:12
  36.8 8.6 %collective-permute-start = (bf16[128,1024]{1,0:T(8,128)(2,1)}, bf16[128,1024]{1,0:T(8,128)(2,1)S(1)}, u32[]{:S(2)}, u32[]{:S(2)}) collective-permute-start(bf16[128,1024]{1,0:T(8,128)(2,1)} %get-tuple-element.216), channel_id=1, source_target_pairs={{0,8},{8,16},{16,24},{1,9},{9,17},{17,25},{2,10},{10,18},{18,26},{... | collective-permute-start | bytes 786440 | tf_op jit(solution)/shard_map/while/body/eval_jaxpr/ppermute | solution.py:12
  40.3 8.6 %collective-permute-start.1 = (bf16[128,1024]{1,0:T(8,128)(2,1)}, bf16[128,1024]{1,0:T(8,128)(2,1)}, u32[]{:S(2)}, u32[]{:S(2)}) collective-permute-start(bf16[128,1024]{1,0:T(8,128)(2,1)} %get-tuple-element.217), channel_id=1, source_target_pairs={{0,2},{2,4},{4,6},{1,3},{3,5},{5,7},{8,10},{10,12},{12,14},{9,11},... | collective-permute-start | bytes 786440 | tf_op jit(solution)/shard_map/while/body/eval_jaxpr/ppermute | solution.py:12
  54.6 8.6 %collective-permute-start = (bf16[128,1024]{1,0:T(8,128)(2,1)}, bf16[128,1024]{1,0:T(8,128)(2,1)S(1)}, u32[]{:S(2)}, u32[]{:S(2)}) collective-permute-start(bf16[128,1024]{1,0:T(8,128)(2,1)} %get-tuple-element.216), channel_id=1, source_target_pairs={{0,8},{8,16},{16,24},{1,9},{9,17},{17,25},{2,10},{10,18},{18,26},{... | collective-permute-start | bytes 786440 | tf_op jit(solution)/shard_map/while/body/eval_jaxpr/ppermute | solution.py:12
  58.1 8.6 %collective-permute-start.1 = (bf16[128,1024]{1,0:T(8,128)(2,1)}, bf16[128,1024]{1,0:T(8,128)(2,1)}, u32[]{:S(2)}, u32[]{:S(2)}) collective-permute-start(bf16[128,1024]{1,0:T(8,128)(2,1)} %get-tuple-element.217), channel_id=1, source_target_pairs={{0,2},{2,4},{4,6},{1,3},{3,5},{5,7},{8,10},{10,12},{12,14},{9,11},... | collective-permute-start | bytes 786440 | tf_op jit(solution)/shard_map/while/body/eval_jaxpr/ppermute | solution.py:12
  72.4 7.8 %collective-permute-start = (bf16[128,1024]{1,0:T(8,128)(2,1)}, bf16[128,1024]{1,0:T(8,128)(2,1)S(1)}, u32[]{:S(2)}, u32[]{:S(2)}) collective-permute-start(bf16[128,1024]{1,0:T(8,128)(2,1)} %get-tuple-element.216), channel_id=1, source_target_pairs={{0,8},{8,16},{16,24},{1,9},{9,17},{17,25},{2,10},{10,18},{18,26},{... | collective-permute-start | bytes 786440 | tf_op jit(solution)/shard_map/while/body/eval_jaxpr/ppermute | solution.py:12
  74.3 9.4 %collective-permute-start.1 = (bf16[128,1024]{1,0:T(8,128)(2,1)}, bf16[128,1024]{1,0:T(8,128)(2,1)}, u32[]{:S(2)}, u32[]{:S(2)}) collective-permute-start(bf16[128,1024]{1,0:T(8,128)(2,1)} %get-tuple-element.217), channel_id=1, source_target_pairs={{0,2},{2,4},{4,6},{1,3},{3,5},{5,7},{8,10},{10,12},{12,14},{9,11},... | collective-permute-start | bytes 786440 | tf_op jit(solution)/shard_map/while/body/eval_jaxpr/ppermute | solution.py:12
  89.4 7.9 %collective-permute-start = (bf16[128,1024]{1,0:T(8,128)(2,1)}, bf16[128,1024]{1,0:T(8,128)(2,1)S(1)}, u32[]{:S(2)}, u32[]{:S(2)}) collective-permute-start(bf16[128,1024]{1,0:T(8,128)(2,1)} %get-tuple-element.216), channel_id=1, source_target_pairs={{0,8},{8,16},{16,24},{1,9},{9,17},{17,25},{2,10},{10,18},{18,26},{... | collective-permute-start | bytes 786440 | tf_op jit(solution)/shard_map/while/body/eval_jaxpr/ppermute | solution.py:12
  91.3 9.5 %collective-permute-start.1 = (bf16[128,1024]{1,0:T(8,128)(2,1)}, bf16[128,1024]{1,0:T(8,128)(2,1)}, u32[]{:S(2)}, u32[]{:S(2)}) collective-permute-start(bf16[128,1024]{1,0:T(8,128)(2,1)} %get-tuple-element.217), channel_id=1, source_target_pairs={{0,2},{2,4},{4,6},{1,3},{3,5},{5,7},{8,10},{10,12},{12,14},{9,11},... | collective-permute-start | bytes 786440 | tf_op jit(solution)/shard_map/while/body/eval_jaxpr/ppermute | solution.py:12
  106.5 7.9 %collective-permute-start = (bf16[128,1024]{1,0:T(8,128)(2,1)}, bf16[128,1024]{1,0:T(8,128)(2,1)S(1)}, u32[]{:S(2)}, u32[]{:S(2)}) collective-permute-start(bf16[128,1024]{1,0:T(8,128)(2,1)} %get-tuple-element.216), channel_id=1, source_target_pairs={{0,8},{8,16},{16,24},{1,9},{9,17},{17,25},{2,10},{10,18},{18,26},{... | collective-permute-start | bytes 786440 | tf_op jit(solution)/shard_map/while/body/eval_jaxpr/ppermute | solution.py:12
  108.5 9.5 %collective-permute-start.1 = (bf16[128,1024]{1,0:T(8,128)(2,1)}, bf16[128,1024]{1,0:T(8,128)(2,1)}, u32[]{:S(2)}, u32[]{:S(2)}) collective-permute-start(bf16[128,1024]{1,0:T(8,128)(2,1)} %get-tuple-element.217), channel_id=1, source_target_pairs={{0,2},{2,4},{4,6},{1,3},{3,5},{5,7},{8,10},{10,12},{12,14},{9,11},... | collective-permute-start | bytes 786440 | tf_op jit(solution)/shard_map/while/body/eval_jaxpr/ppermute | solution.py:12
  123.7 7.9 %collective-permute-start = (bf16[128,1024]{1,0:T(8,128)(2,1)}, bf16[128,1024]{1,0:T(8,128)(2,1)S(1)}, u32[]{:S(2)}, u32[]{:S(2)}) collective-permute-start(bf16[128,1024]{1,0:T(8,128)(2,1)} %get-tuple-element.216), channel_id=1, source_target_pairs={{0,8},{8,16},{16,24},{1,9},{9,17},{17,25},{2,10},{10,18},{18,26},{... | collective-permute-start | bytes 786440 | tf_op jit(solution)/shard_map/while/body/eval_jaxpr/ppermute | solution.py:12
  125.6 9.5 %collective-permute-start.1 = (bf16[128,1024]{1,0:T(8,128)(2,1)}, bf16[128,1024]{1,0:T(8,128)(2,1)}, u32[]{:S(2)}, u32[]{:S(2)}) collective-permute-start(bf16[128,1024]{1,0:T(8,128)(2,1)} %get-tuple-element.217), channel_id=1, source_target_pairs={{0,2},{2,4},{4,6},{1,3},{3,5},{5,7},{8,10},{10,12},{12,14},{9,11},... | collective-permute-start | bytes 786440 | tf_op jit(solution)/shard_map/while/body/eval_jaxpr/ppermute | solution.py:12
  140.8 7.9 %collective-permute-start = (bf16[128,1024]{1,0:T(8,128)(2,1)}, bf16[128,1024]{1,0:T(8,128)(2,1)S(1)}, u32[]{:S(2)}, u32[]{:S(2)}) collective-permute-start(bf16[128,1024]{1,0:T(8,128)(2,1)} %get-tuple-element.216), channel_id=1, source_target_pairs={{0,8},{8,16},{16,24},{1,9},{9,17},{17,25},{2,10},{10,18},{18,26},{... | collective-permute-start | bytes 786440 | tf_op jit(solution)/shard_map/while/body/eval_jaxpr/ppermute | solution.py:12
  142.7 9.6 %collective-permute-start.1 = (bf16[128,1024]{1,0:T(8,128)(2,1)}, bf16[128,1024]{1,0:T(8,128)(2,1)}, u32[]{:S(2)}, u32[]{:S(2)}) collective-permute-start(bf16[128,1024]{1,0:T(8,128)(2,1)} %get-tuple-element.217), channel_id=1, source_target_pairs={{0,2},{2,4},{4,6},{1,3},{3,5},{5,7},{8,10},{10,12},{12,14},{9,11},... | collective-permute-start | bytes 786440 | tf_op jit(solution)/shard_map/while/body/eval_jaxpr/ppermute | solution.py:12
  152.3 13.1 %copy-start = (bf16[256,2048]{1,0:T(8,128)(2,1)}, bf16[256,2048]{1,0:T(8,128)(2,1)S(1)}, u32[]{:S(2)}) copy-start(bf16[256,2048]{1,0:T(8,128)(2,1)S(1)} %get-tuple-element.141) | copy-start | bytes 3145732
  153.4 11.2 %all-to-all-start.1 = ((bf16[4,8,256]{2,1,0:T(8,128)(2,1)}), bf16[4,8,256]{2,1,0:T(8,128)(2,1)S(1)}, u32[]{:S(2)}, u32[]{:S(2)}) async-start(bf16[4,8,256]{2,1,0:T(8,128)(2,1)} %fusion.6), calls=%async_computation.1 | async-start | bytes 32768 | tf_op jit(solution)/shard_map/all_to_all | solution.py:78
where the time goes:
time: 166 us; the launch traced here: 165 us
  starting transfers between devices  76.3 us (46%)
  matrix products  41.1 us (25%)
  waiting for transfers between devices  33.4 us (20%)
  local copies, waits for them, and re-layouts  8.17 us (5%)
  other arithmetic  5.61 us (3%)
    ppermute x16, starting transfers between devices, passed_along(): return lax.ppermute(shard, axis, pairs)  64.7 us
    dot_general x8, matrix products, advance(): jnp.dot(joined, matrix, preferred_element_type=jnp.float32)  39.2 us
    ppermute x16, waiting for transfers between devices, passed_along(): return lax.ppermute(shard, axis, pairs)  28.8 us
    slice x8, local copies, waits for them, and re-layouts, advance(): right_next = passed_along(update[:, half:], 'col', 1)  6.53 us
    all_to_all x1, starting transfers between devices, on_device(): lax.all_to_all(packed, 'col', split_axis=0, concat_axis=0, tiled=True)  6.46 us
    all_to_all x1, starting transfers between devices, on_device(): lax.all_to_all(slot_rows, 'col', split_axis=0, concat_axis=0, tiled=True)  5.16 us
    all_to_all x1, waiting for transfers between devices, on_device(): lax.all_to_all(packed, 'col', split_axis=0, concat_axis=0, tiled=True)  4.61 us
  transfers between devices with their start and end apart: 18, of which 10 were waited for; matrix products, arithmetic and copies ran while one was open for 30% of the time, Pallas kernels for 0%

commit v1 on v0

v1 whole, which is shorter than its diff:
```python
import jax
import jax.numpy as jnp
from jax import lax
from jax.sharding import PartitionSpec as P

DB = 128
BLOCKS = 2
ORDER = 'rl'


def passed_along(shard, axis, by):
    peers = lax.axis_size(axis)
    pairs = [(i, i + by) for i in range(peers) if 0 <= i + by < peers]
    return lax.ppermute(shard, axis, pairs)


def on_device(green, background, wavelet, station_cell, fault_point, fault_owner, fault_row):
    row_place = lax.axis_index("row")
    col_place = lax.axis_index("col")
    row_count = lax.axis_size("row")
    col_count = lax.axis_size("col")
    matrix = green[0, 0]
    half = matrix.shape[0] // 2
    stations = background.shape[2]
    own_source = (station_cell == row_place * col_count + col_place)[:, None]
    source = background[0, 0].astype(jnp.float32) + jnp.where(
        own_source, wavelet.astype(jnp.float32), 0.0
    )
    height = stations // BLOCKS
    total_fronts = row_count + col_count + BLOCKS - 2
    down_in = jnp.zeros((height, half), jnp.bfloat16)
    right_in = jnp.zeros((height, half), jnp.bfloat16)
    field = jnp.zeros((stations, 2 * half), jnp.bfloat16)
    for moment in range(total_fronts):
        block = moment - row_place - col_place
        active = jnp.logical_and(block >= 0, block < BLOCKS)
        start = jnp.clip(block, 0, BLOCKS - 1) * height
        part = lax.dynamic_slice_in_dim(source, start, height, 0)
        joined = jnp.concatenate([down_in, right_in], axis=1)
        if ORDER == "one":
            update = (jnp.dot(joined, matrix, preferred_element_type=jnp.float32) + part).astype(jnp.bfloat16)
            lower, right = update[:, :half], update[:, half:]
            right_next = passed_along(right, "col", 1)
            down_next = passed_along(lower, "row", 1)
        else:
            def face(lo):
                cols = slice(0, half) if lo else slice(half, 2 * half)
                return (jnp.dot(joined, matrix[:, cols], preferred_element_type=jnp.float32) + part[:, cols]).astype(jnp.bfloat16)
            if ORDER == "rl":
                right = face(False)
                right_next = passed_along(right, "col", 1)
                lower = face(True)
                down_next = passed_along(lower, "row", 1)
            else:
                lower = face(True)
                down_next = passed_along(lower, "row", 1)
                right = face(False)
                right_next = passed_along(right, "col", 1)
            update = jnp.concatenate([lower, right], axis=1)
        previous = lax.dynamic_slice_in_dim(field, start, height, 0)
        field = lax.dynamic_update_slice_in_dim(field, jnp.where(active, update, previous), start, 0)
        down_in, right_in = down_next, right_next
    points = fault_point[0]
    owners = fault_owner[0, :, 0]
    targets = fault_row[0]
    listed = points.shape[0]
    point_hot = (points[:, None] == jnp.arange(2 * half, dtype=jnp.int32)[None, :]).astype(jnp.bfloat16)
    traces = jnp.einsum("qp,sp->qs", point_hot, field, preferred_element_type=jnp.float32).astype(jnp.bfloat16)
    capacity = 2 * listed // col_count
    owner_hot = (owners[:, None] == jnp.arange(col_count, dtype=jnp.int32)[None, :]).astype(jnp.int32)
    running = jnp.cumsum(owner_hot, axis=0) - 1
    rank = jnp.sum(owner_hot * running, axis=1)
    slots = owners * capacity + rank
    slot_match = slots[None, :] == jnp.arange(col_count * capacity, dtype=jnp.int32)[:, None]
    slot_hot = slot_match.astype(jnp.bfloat16)
    packed = jnp.dot(slot_hot, traces, preferred_element_type=jnp.float32).astype(jnp.bfloat16)
    slot_rows = jnp.sum(jnp.where(slot_match, targets[None, :] + 1, 0), axis=1) - 1
    tag = jnp.broadcast_to(slot_rows.astype(jnp.bfloat16)[:, None], (col_count * capacity, 128))
    message = jnp.concatenate([packed, tag], axis=1).reshape(col_count, capacity, stations + 128)
    arrived = lax.all_to_all(message, "col", split_axis=0, concat_axis=0, tiled=True)
    arrived = arrived.reshape(col_count * capacity, stations + 128)
    row_numbers = arrived[:, stations].astype(jnp.int32)
    table_hot = (row_numbers[None, :] == jnp.arange(DB, dtype=jnp.int32)[:, None]).astype(jnp.bfloat16)
    database = jnp.dot(table_hot, arrived[:, :stations], preferred_element_type=jnp.float32)
    return (field[None, None], database[None, None])


def solution(mesh):
    in_specs = (
        P("row", "col", None, None),
        P("row", "col", "batch", None),
        P("batch", None),
        P("batch"),
        P("row", "col"),
        P("row", "col", None),
        P("row", "col"),
    )
    out_specs = (P("row", "col", "batch", None), P("row", "col", None, "batch"))
    return jax.shard_map(
        on_device, mesh=mesh, in_specs=in_specs, out_specs=out_specs, check_vma=False
    )
```

time: 166 us -> 122 us (0.73)
  starting transfers between devices: 76.3 us -> 54.2 us
  matrix products: 41.1 us -> 22.9 us
  blocking collectives: 0 us -> 11.2 us
  waiting for transfers between devices: 33.4 us -> 24.2 us
  local copies, waits for them, and re-layouts: 8.17 us -> 2.38 us
    dot_general x9 -> x17, matrix products: 40 us -> 22.4 us  [the longest x16 21.6 us: face(): jnp.dot(joined, matrix[:, cols], preferred_element_type=jnp.float32)]
    all_to_all x2 -> x0, starting transfers between devices: 11.6 us -> none  [the longest x1 6.46 us: on_device(): lax.all_to_all(packed, 'col', split_axis=0, concat_axis=0, tiled=True)]
    all_to_all x0 -> x1, blocking collectives: none -> 11.2 us  [on_device(): lax.all_to_all(message, 'col', split_axis=0, concat_axis=0, tiled=True)]
    ppermute x16 -> x14, starting transfers between devices: 64.7 us -> 54.2 us  [passed_along(): return lax.ppermute(shard, axis, pairs)]
    slice x8 -> x0, local copies, waits for them, and re-layouts: 6.53 us -> none  [advance(): right_next = passed_along(update[:, half:], 'col', 1)]
    all_to_all x2 -> x0, waiting for transfers between devices: 4.61 us -> none  [the longest x1 4.61 us: on_device(): lax.all_to_all(packed, 'col', split_axis=0, concat_axis=0, tiled=True)]
    ppermute x16 -> x14, waiting for transfers between devices: 28.8 us -> 24.2 us  [passed_along(): return lax.ppermute(shard, axis, pairs)]
    dynamic_update_slice x0 -> x8, other arithmetic: none -> 2.37 us  [on_device(): lax.dynamic_update_slice_in_dim(field, jnp.where(active, update, previous...]
  transfers between devices with their start and end apart: 18 -> 14, of which waited for: 10 -> 7; matrix products, arithmetic and copies ran while one was open for 30% -> 12% of each run, Pallas kernels for 0% -> 0%
where the time goes in v1:
time: 122 us; the launch traced here: 121 us
  starting transfers between devices  54.2 us (44%)
  waiting for transfers between devices  24.2 us (20%)
  matrix products  22.9 us (19%)
  blocking collectives  11.2 us (9%)
  other arithmetic  5.46 us (4%)
  local copies, waits for them, and re-layouts  2.38 us (2%)
    ppermute x14, starting transfers between devices, passed_along(): return lax.ppermute(shard, axis, pairs)  54.2 us
    ppermute x14, waiting for transfers between devices, passed_along(): return lax.ppermute(shard, axis, pairs)  24.2 us
    dot_general x16, matrix products, face(): jnp.dot(joined, matrix[:, cols], preferred_element_type=jnp.float32)  21.6 us
    all_to_all x1, blocking collectives, on_device(): lax.all_to_all(message, 'col', split_axis=0, concat_axis=0, tiled=True)  11.2 us
  transfers between devices with their start and end apart: 14, of which 7 were waited for; matrix products, arithmetic and copies ran while one was open for 12% of the time, Pallas kernels for 0%

profile of v1, /device:TPU:0, one launch (start us, length us, event | category | flops | bytes accessed | tf_op | source)
XLA Modules:
  0.0 121.5 jit_solution(12399657545033652843)
XLA Ops:
  1.3 1.9 %convert_add_fusion = f32[256,2048]{1,0:T(8,128)S(1)} fusion(bf16[256,2048]{1,0:T(8,128)(2,1)} %param.9, bf16[1,1,256,2048]{3,2,1,0:T(8,128)(2,1)} %param.8, pred[256]{0:T(512)(128)(4,1)S(1)} %broadcast_compare_fusion), kind=kLoop, calls=%fused_computation | loop fusion | flops 2097152 | bytes 4194560 | tf_op jit(solution)/shard_map/add | solution.py:26
  3.2 2.9 %fusion = bf16[128,1024]{1,0:T(8,128)(2,1)S(1)} fusion(bf16[2048,2048]{1,0:T(8,128)(2,1)} %bitcast.36, f32[256,2048]{1,0:T(8,128)S(1)} %convert_add_fusion, s32[]{:T(128)S(6)} %select_n.99), kind=kOutput, calls=%fused_computation.17 | convolution fusion | flops 537133056 | bytes 4980740 | tf_op jit(solution)/shard_map/dot_general | solution.py:48
  6.2 5.7 %collective-permute-start = (bf16[128,1024]{1,0:T(8,128)(2,1)S(1)}, bf16[128,1024]{1,0:T(8,128)(2,1)}, u32[]{:S(2)}, u32[]{:S(2)}) collective-permute-start(bf16[128,1024]{1,0:T(8,128)(2,1)S(1)} %fusion), channel_id=1, source_target_pairs={{0,8},{8,16},{16,24},{1,9},{9,17},{17,25},{2,10},{10,18},{18,26},{... | collective-permute-start | bytes 786440 | tf_op jit(solution)/shard_map/ppermute | solution.py:14
  11.8 3.6 %fusion.1 = bf16[128,1024]{1,0:T(8,128)(2,1)} fusion(bf16[2048,2048]{1,0:T(8,128)(2,1)} %bitcast.37, f32[256,2048]{1,0:T(8,128)S(1)} %convert_add_fusion, s32[]{:T(128)S(6)} %select_n.99, s32[]{:T(128)S(6)} %add.138), kind=kOutput, calls=%fused_computation.18 | convolution fusion | flops 537133056 | bytes 4980744 | tf_op jit(solution)/shard_map/dot_general | solution.py:48
  15.4 4.1 %collective-permute-start.1 = (bf16[128,1024]{1,0:T(8,128)(2,1)}, bf16[128,1024]{1,0:T(8,128)(2,1)}, u32[]{:S(2)}, u32[]{:S(2)}) collective-permute-start(bf16[128,1024]{1,0:T(8,128)(2,1)} %fusion.1), channel_id=1, source_target_pairs={{0,2},{2,4},{4,6},{1,3},{3,5},{5,7},{8,10},{10,12},{12,14},{9,11},... | collective-permute-start | bytes 786440 | tf_op jit(solution)/shard_map/ppermute | solution.py:14
  19.9 1.1 fusion.32
  21.2 1.0 constant_dynamic-update-slice_fusion.1
  22.1 2.2 %collective-permute-done.1 = bf16[128,1024]{1,0:T(8,128)(2,1)} collective-permute-done((bf16[128,1024]{1,0:T(8,128)(2,1)}, bf16[128,1024]{1,0:T(8,128)(2,1)}, u32[]{:S(2)}, u32[]{:S(2)}) %collective-permute-start.1) | collective-permute-done | bytes 262176 | tf_op jit(solution)/shard_map/ppermute | solution.py:14
  24.4 1.0 constant_dynamic-update-slice_fusion
  25.4 3.1 %fusion.2 = bf16[128,1024]{1,0:T(8,128)(2,1)S(1)} fusion(bf16[128,2048]{1,0:T(8,128)(2,1)S(1)} %constant_dynamic-update-slice_fusion, bf16[2048,2048]{1,0:T(8,128)(2,1)} %bitcast.38, f32[256,2048]{1,0:T(8,128)S(1)} %convert_add_fusion, s32[]{:T(128)S(6)} %select_n.102), kind=kOutput, calls=%fused_computation.19 | convolution fusion | flops 537133056 | bytes 5505028 | tf_op jit(solution)/shard_map/dot_general | solution.py:48
  28.5 3.1 %collective-permute-start.2 = (bf16[128,1024]{1,0:T(8,128)(2,1)S(1)}, bf16[128,1024]{1,0:T(8,128)(2,1)S(1)}, u32[]{:S(2)}, u32[]{:S(2)}) collective-permute-start(bf16[128,1024]{1,0:T(8,128)(2,1)S(1)} %fusion.2), channel_id=1, source_target_pairs={{0,8},{8,16},{16,24},{1,9},{9,17},{17,25},{2,10},{10,18},{18,26},{... | collective-permute-start | bytes 786440 | tf_op jit(solution)/shard_map/ppermute | solution.py:14
  31.6 2.9 %fusion.3 = bf16[128,1024]{1,0:T(8,128)(2,1)S(1)} fusion(bf16[128,2048]{1,0:T(8,128)(2,1)S(1)} %constant_dynamic-update-slice_fusion, bf16[2048,2048]{1,0:T(8,128)(2,1)} %bitcast.39, f32[256,2048]{1,0:T(8,128)S(1)} %convert_add_fusion, s32[]{:T(128)S(6)} %select_n.102, s32[]{:T(128)S(6)} %add.138), kind=kOutput, calls=%fused_computation.20 | convolution fusion | flops 537133056 | bytes 5505032 | tf_op jit(solution)/shard_map/dot_general | solution.py:48
  34.5 4.4 %collective-permute-start.3 = (bf16[128,1024]{1,0:T(8,128)(2,1)S(1)}, bf16[128,1024]{1,0:T(8,128)(2,1)S(1)}, u32[]{:S(2)}, u32[]{:S(2)}) collective-permute-start(bf16[128,1024]{1,0:T(8,128)(2,1)S(1)} %fusion.3), channel_id=1, source_target_pairs={{0,2},{2,4},{4,6},{1,3},{3,5},{5,7},{8,10},{10,12},{12,14},{9,11},... | collective-permute-start | bytes 786440 | tf_op jit(solution)/shard_map/ppermute | solution.py:14
  39.2 3.8 %collective-permute-done.3 = bf16[128,1024]{1,0:T(8,128)(2,1)S(1)} collective-permute-done((bf16[128,1024]{1,0:T(8,128)(2,1)S(1)}, bf16[128,1024]{1,0:T(8,128)(2,1)S(1)}, u32[]{:S(2)}, u32[]{:S(2)}) %collective-permute-start.3) | collective-permute-done | bytes 262176 | tf_op jit(solution)/shard_map/ppermute | solution.py:14
  43.8 3.5 %collective-permute-start.4 = (bf16[128,1024]{1,0:T(8,128)(2,1)S(1)}, bf16[128,1024]{1,0:T(8,128)(2,1)S(1)}, u32[]{:S(2)}, u32[]{:S(2)}) collective-permute-start(bf16[128,1024]{1,0:T(8,128)(2,1)S(1)} %fusion.4), channel_id=1, source_target_pairs={{0,8},{8,16},{16,24},{1,9},{9,17},{17,25},{2,10},{10,18},{18,26},{... | collective-permute-start | bytes 786440 | tf_op jit(solution)/shard_map/ppermute | solution.py:14
  48.0 4.4 %collective-permute-start.5 = (bf16[128,1024]{1,0:T(8,128)(2,1)S(1)}, bf16[128,1024]{1,0:T(8,128)(2,1)S(1)}, u32[]{:S(2)}, u32[]{:S(2)}) collective-permute-start(bf16[128,1024]{1,0:T(8,128)(2,1)S(1)} %fusion.5), channel_id=1, source_target_pairs={{0,2},{2,4},{4,6},{1,3},{3,5},{5,7},{8,10},{10,12},{12,14},{9,11},... | collective-permute-start | bytes 786440 | tf_op jit(solution)/shard_map/ppermute | solution.py:14
  52.7 3.6 %collective-permute-done.5 = bf16[128,1024]{1,0:T(8,128)(2,1)S(1)} collective-permute-done((bf16[128,1024]{1,0:T(8,128)(2,1)S(1)}, bf16[128,1024]{1,0:T(8,128)(2,1)S(1)}, u32[]{:S(2)}, u32[]{:S(2)}) %collective-permute-start.5) | collective-permute-done | bytes 262176 | tf_op jit(solution)/shard_map/ppermute | solution.py:14
  57.1 2.2 %collective-permute-start.6 = (bf16[128,1024]{1,0:T(8,128)(2,1)S(1)}, bf16[128,1024]{1,0:T(8,128)(2,1)S(1)}, u32[]{:S(2)}, u32[]{:S(2)}) collective-permute-start(bf16[128,1024]{1,0:T(8,128)(2,1)S(1)} %fusion.6), channel_id=1, source_target_pairs={{0,8},{8,16},{16,24},{1,9},{9,17},{17,25},{2,10},{10,18},{18,26},{... | collective-permute-start | bytes 786440 | tf_op jit(solution)/shard_map/ppermute | solution.py:14
  60.0 5.2 %collective-permute-start.7 = (bf16[128,1024]{1,0:T(8,128)(2,1)S(1)}, bf16[128,1024]{1,0:T(8,128)(2,1)S(1)}, u32[]{:S(2)}, u32[]{:S(2)}) collective-permute-start(bf16[128,1024]{1,0:T(8,128)(2,1)S(1)} %fusion.7), channel_id=1, source_target_pairs={{0,2},{2,4},{4,6},{1,3},{3,5},{5,7},{8,10},{10,12},{12,14},{9,11},... | collective-permute-start | bytes 786440 | tf_op jit(solution)/shard_map/ppermute | solution.py:14
  65.5 3.6 %collective-permute-done.7 = bf16[128,1024]{1,0:T(8,128)(2,1)S(1)} collective-permute-done((bf16[128,1024]{1,0:T(8,128)(2,1)S(1)}, bf16[128,1024]{1,0:T(8,128)(2,1)S(1)}, u32[]{:S(2)}, u32[]{:S(2)}) %collective-permute-start.7) | collective-permute-done | bytes 262176 | tf_op jit(solution)/shard_map/ppermute | solution.py:14
  69.9 1.9 %collective-permute-start.8 = (bf16[128,1024]{1,0:T(8,128)(2,1)S(1)}, bf16[128,1024]{1,0:T(8,128)(2,1)S(1)}, u32[]{:S(2)}, u32[]{:S(2)}) collective-permute-start(bf16[128,1024]{1,0:T(8,128)(2,1)S(1)} %fusion.8), channel_id=1, source_target_pairs={{0,8},{8,16},{16,24},{1,9},{9,17},{17,25},{2,10},{10,18},{18,26},{... | collective-permute-start | bytes 786440 | tf_op jit(solution)/shard_map/ppermute | solution.py:14
  71.8 0.8 fusion.9
  72.6 5.3 %collective-permute-start.9 = (bf16[128,1024]{1,0:T(8,128)(2,1)S(1)}, bf16[128,1024]{1,0:T(8,128)(2,1)S(1)}, u32[]{:S(2)}, u32[]{:S(2)}) collective-permute-start(bf16[128,1024]{1,0:T(8,128)(2,1)S(1)} %fusion.9), channel_id=1, source_target_pairs={{0,2},{2,4},{4,6},{1,3},{3,5},{5,7},{8,10},{10,12},{12,14},{9,11},... | collective-permute-start | bytes 786440 | tf_op jit(solution)/shard_map/ppermute | solution.py:14
  78.1 3.6 %collective-permute-done.9 = bf16[128,1024]{1,0:T(8,128)(2,1)S(1)} collective-permute-done((bf16[128,1024]{1,0:T(8,128)(2,1)S(1)}, bf16[128,1024]{1,0:T(8,128)(2,1)S(1)}, u32[]{:S(2)}, u32[]{:S(2)}) %collective-permute-start.9) | collective-permute-done | bytes 262176 | tf_op jit(solution)/shard_map/ppermute | solution.py:14
  82.5 1.9 %collective-permute-start.10 = (bf16[128,1024]{1,0:T(8,128)(2,1)S(1)}, bf16[128,1024]{1,0:T(8,128)(2,1)S(1)}, u32[]{:S(2)}, u32[]{:S(2)}) collective-permute-start(bf16[128,1024]{1,0:T(8,128)(2,1)S(1)} %fusion.10), channel_id=1, source_target_pairs={{0,8},{8,16},{16,24},{1,9},{9,17},{17,25},{2,10},{10,18},{18,26},{... | collective-permute-start | bytes 786440 | tf_op jit(solution)/shard_map/ppermute | solution.py:14
  85.2 5.3 %collective-permute-start.11 = (bf16[128,1024]{1,0:T(8,128)(2,1)S(1)}, bf16[128,1024]{1,0:T(8,128)(2,1)S(1)}, u32[]{:S(2)}, u32[]{:S(2)}) collective-permute-start(bf16[128,1024]{1,0:T(8,128)(2,1)S(1)} %fusion.11), channel_id=1, source_target_pairs={{0,2},{2,4},{4,6},{1,3},{3,5},{5,7},{8,10},{10,12},{12,14},{9,11},... | collective-permute-start | bytes 786440 | tf_op jit(solution)/shard_map/ppermute | solution.py:14
  90.7 3.6 %collective-permute-done.11 = bf16[128,1024]{1,0:T(8,128)(2,1)S(1)} collective-permute-done((bf16[128,1024]{1,0:T(8,128)(2,1)S(1)}, bf16[128,1024]{1,0:T(8,128)(2,1)S(1)}, u32[]{:S(2)}, u32[]{:S(2)}) %collective-permute-start.11) | collective-permute-done | bytes 262176 | tf_op jit(solution)/shard_map/ppermute | solution.py:14
  95.1 1.9 %collective-permute-start.12 = (bf16[128,1024]{1,0:T(8,128)(2,1)S(1)}, bf16[128,1024]{1,0:T(8,128)(2,1)S(1)}, u32[]{:S(2)}, u32[]{:S(2)}) collective-permute-start(bf16[128,1024]{1,0:T(8,128)(2,1)S(1)} %fusion.12), channel_id=1, source_target_pairs={{0,8},{8,16},{16,24},{1,9},{9,17},{17,25},{2,10},{10,18},{18,26},{... | collective-permute-start | bytes 786440 | tf_op jit(solution)/shard_map/ppermute | solution.py:14
  97.8 5.3 %collective-permute-start.13 = (bf16[128,1024]{1,0:T(8,128)(2,1)S(1)}, bf16[128,1024]{1,0:T(8,128)(2,1)S(1)}, u32[]{:S(2)}, u32[]{:S(2)}) collective-permute-start(bf16[128,1024]{1,0:T(8,128)(2,1)S(1)} %fusion.13), channel_id=1, source_target_pairs={{0,2},{2,4},{4,6},{1,3},{3,5},{5,7},{8,10},{10,12},{12,14},{9,11},... | collective-permute-start | bytes 786440 | tf_op jit(solution)/shard_map/ppermute | solution.py:14
  103.4 3.6 %collective-permute-done.13 = bf16[128,1024]{1,0:T(8,128)(2,1)S(1)} collective-permute-done((bf16[128,1024]{1,0:T(8,128)(2,1)S(1)}, bf16[128,1024]{1,0:T(8,128)(2,1)S(1)}, u32[]{:S(2)}, u32[]{:S(2)}) %collective-permute-start.13) | collective-permute-done | bytes 262176 | tf_op jit(solution)/shard_map/ppermute | solution.py:14
  109.3 11.2 %all_to_all.5 = bf16[4,8,384]{2,1,0:T(8,128)(2,1)S(1)} all-to-all(bf16[4,8,384]{2,1,0:T(8,128)(2,1)S(1)} %maximum_bitcast_fusion), channel_id=1, replica_groups=mesh['row'=4,'col'=4,'batch'=2] {'col'}, dimensions={0} | all-to-all | bytes 49152 | tf_op jit(solution)/shard_map/all_to_all | solution.py:80
  120.7 0.8 convolution_bitcast_fusion
  (63 shorter events, 11.7 us)
Async XLA Ops:
  6.1 13.4 %copy-start.3 = (s32[1,16]{1,0:T(1,128)S(1)}, s32[1,16]{1,0:T(1,128)}, u32[]{:S(2)}) copy-start(s32[1,16]{1,0:T(1,128)} %param.13) | copy-start | bytes 196
  6.1 13.4 %copy-start.1 = (s32[1,16,1]{1,2,0:T(1,128)S(1)}, s32[1,16,1]{1,2,0:T(1,128)}, u32[]{:S(2)}) copy-start(s32[1,16,1]{1,2,0:T(1,128)} %param.12) | copy-start | bytes 196
  6.2 15.0 %collective-permute-start = (bf16[128,1024]{1,0:T(8,128)(2,1)S(1)}, bf16[128,1024]{1,0:T(8,128)(2,1)}, u32[]{:S(2)}, u32[]{:S(2)}) collective-permute-start(bf16[128,1024]{1,0:T(8,128)(2,1)S(1)} %fusion), channel_id=1, source_target_pairs={{0,8},{8,16},{16,24},{1,9},{9,17},{17,25},{2,10},{10,18},{18,26},{... | collective-permute-start | bytes 786440 | tf_op jit(solution)/shard_map/ppermute | solution.py:14
  15.4 9.0 %collective-permute-start.1 = (bf16[128,1024]{1,0:T(8,128)(2,1)}, bf16[128,1024]{1,0:T(8,128)(2,1)}, u32[]{:S(2)}, u32[]{:S(2)}) collective-permute-start(bf16[128,1024]{1,0:T(8,128)(2,1)} %fusion.1), channel_id=1, source_target_pairs={{0,2},{2,4},{4,6},{1,3},{3,5},{5,7},{8,10},{10,12},{12,14},{9,11},... | collective-permute-start | bytes 786440 | tf_op jit(solution)/shard_map/ppermute | solution.py:14
  25.4 17.6 %slice-start = ((s8[8388608]{0:T(1024)(128)(4,1)}), s8[4194304]{0:T(1024)(128)(4,1)S(1)}, s32[]{:S(2)}) async-start(s8[8388608]{0:T(1024)(128)(4,1)} %bitcast.40), calls=%async_computation.1 | async-start | bytes 8388608
  28.5 14.5 %slice-start.1 = ((s8[8388608]{0:T(1024)(128)(4,1)}), s8[4194304]{0:T(1024)(128)(4,1)S(1)}, s32[]{:S(2)}) async-start(s8[8388608]{0:T(1024)(128)(4,1)} %bitcast.40), calls=%async_computation.2 | async-start | bytes 8388608
  28.5 10.6 %collective-permute-start.2 = (bf16[128,1024]{1,0:T(8,128)(2,1)S(1)}, bf16[128,1024]{1,0:T(8,128)(2,1)S(1)}, u32[]{:S(2)}, u32[]{:S(2)}) collective-permute-start(bf16[128,1024]{1,0:T(8,128)(2,1)S(1)} %fusion.2), channel_id=1, source_target_pairs={{0,8},{8,16},{16,24},{1,9},{9,17},{17,25},{2,10},{10,18},{18,26},{... | collective-permute-start | bytes 786440 | tf_op jit(solution)/shard_map/ppermute | solution.py:14
  34.5 8.5 %collective-permute-start.3 = (bf16[128,1024]{1,0:T(8,128)(2,1)S(1)}, bf16[128,1024]{1,0:T(8,128)(2,1)S(1)}, u32[]{:S(2)}, u32[]{:S(2)}) collective-permute-start(bf16[128,1024]{1,0:T(8,128)(2,1)S(1)} %fusion.3), channel_id=1, source_target_pairs={{0,2},{2,4},{4,6},{1,3},{3,5},{5,7},{8,10},{10,12},{12,14},{9,11},... | collective-permute-start | bytes 786440 | tf_op jit(solution)/shard_map/ppermute | solution.py:14
  43.8 8.8 %collective-permute-start.4 = (bf16[128,1024]{1,0:T(8,128)(2,1)S(1)}, bf16[128,1024]{1,0:T(8,128)(2,1)S(1)}, u32[]{:S(2)}, u32[]{:S(2)}) collective-permute-start(bf16[128,1024]{1,0:T(8,128)(2,1)S(1)} %fusion.4), channel_id=1, source_target_pairs={{0,8},{8,16},{16,24},{1,9},{9,17},{17,25},{2,10},{10,18},{18,26},{... | collective-permute-start | bytes 786440 | tf_op jit(solution)/shard_map/ppermute | solution.py:14
  48.0 8.3 %collective-permute-start.5 = (bf16[128,1024]{1,0:T(8,128)(2,1)S(1)}, bf16[128,1024]{1,0:T(8,128)(2,1)S(1)}, u32[]{:S(2)}, u32[]{:S(2)}) collective-permute-start(bf16[128,1024]{1,0:T(8,128)(2,1)S(1)} %fusion.5), channel_id=1, source_target_pairs={{0,2},{2,4},{4,6},{1,3},{3,5},{5,7},{8,10},{10,12},{12,14},{9,11},... | collective-permute-start | bytes 786440 | tf_op jit(solution)/shard_map/ppermute | solution.py:14
  57.1 8.4 %collective-permute-start.6 = (bf16[128,1024]{1,0:T(8,128)(2,1)S(1)}, bf16[128,1024]{1,0:T(8,128)(2,1)S(1)}, u32[]{:S(2)}, u32[]{:S(2)}) collective-permute-start(bf16[128,1024]{1,0:T(8,128)(2,1)S(1)} %fusion.6), channel_id=1, source_target_pairs={{0,8},{8,16},{16,24},{1,9},{9,17},{17,25},{2,10},{10,18},{18,26},{... | collective-permute-start | bytes 786440 | tf_op jit(solution)/shard_map/ppermute | solution.py:14
  60.0 9.1 %collective-permute-start.7 = (bf16[128,1024]{1,0:T(8,128)(2,1)S(1)}, bf16[128,1024]{1,0:T(8,128)(2,1)S(1)}, u32[]{:S(2)}, u32[]{:S(2)}) collective-permute-start(bf16[128,1024]{1,0:T(8,128)(2,1)S(1)} %fusion.7), channel_id=1, source_target_pairs={{0,2},{2,4},{4,6},{1,3},{3,5},{5,7},{8,10},{10,12},{12,14},{9,11},... | collective-permute-start | bytes 786440 | tf_op jit(solution)/shard_map/ppermute | solution.py:14
  69.9 8.2 %collective-permute-start.8 = (bf16[128,1024]{1,0:T(8,128)(2,1)S(1)}, bf16[128,1024]{1,0:T(8,128)(2,1)S(1)}, u32[]{:S(2)}, u32[]{:S(2)}) collective-permute-start(bf16[128,1024]{1,0:T(8,128)(2,1)S(1)} %fusion.8), channel_id=1, source_target_pairs={{0,8},{8,16},{16,24},{1,9},{9,17},{17,25},{2,10},{10,18},{18,26},{... | collective-permute-start | bytes 786440 | tf_op jit(solution)/shard_map/ppermute | solution.py:14
  72.6 9.2 %collective-permute-start.9 = (bf16[128,1024]{1,0:T(8,128)(2,1)S(1)}, bf16[128,1024]{1,0:T(8,128)(2,1)S(1)}, u32[]{:S(2)}, u32[]{:S(2)}) collective-permute-start(bf16[128,1024]{1,0:T(8,128)(2,1)S(1)} %fusion.9), channel_id=1, source_target_pairs={{0,2},{2,4},{4,6},{1,3},{3,5},{5,7},{8,10},{10,12},{12,14},{9,11},... | collective-permute-start | bytes 786440 | tf_op jit(solution)/shard_map/ppermute | solution.py:14
  82.5 8.2 %collective-permute-start.10 = (bf16[128,1024]{1,0:T(8,128)(2,1)S(1)}, bf16[128,1024]{1,0:T(8,128)(2,1)S(1)}, u32[]{:S(2)}, u32[]{:S(2)}) collective-permute-start(bf16[128,1024]{1,0:T(8,128)(2,1)S(1)} %fusion.10), channel_id=1, source_target_pairs={{0,8},{8,16},{16,24},{1,9},{9,17},{17,25},{2,10},{10,18},{18,26},{... | collective-permute-start | bytes 786440 | tf_op jit(solution)/shard_map/ppermute | solution.py:14
  85.2 9.2 %collective-permute-start.11 = (bf16[128,1024]{1,0:T(8,128)(2,1)S(1)}, bf16[128,1024]{1,0:T(8,128)(2,1)S(1)}, u32[]{:S(2)}, u32[]{:S(2)}) collective-permute-start(bf16[128,1024]{1,0:T(8,128)(2,1)S(1)} %fusion.11), channel_id=1, source_target_pairs={{0,2},{2,4},{4,6},{1,3},{3,5},{5,7},{8,10},{10,12},{12,14},{9,11},... | collective-permute-start | bytes 786440 | tf_op jit(solution)/shard_map/ppermute | solution.py:14
  95.1 8.2 %collective-permute-start.12 = (bf16[128,1024]{1,0:T(8,128)(2,1)S(1)}, bf16[128,1024]{1,0:T(8,128)(2,1)S(1)}, u32[]{:S(2)}, u32[]{:S(2)}) collective-permute-start(bf16[128,1024]{1,0:T(8,128)(2,1)S(1)} %fusion.12), channel_id=1, source_target_pairs={{0,8},{8,16},{16,24},{1,9},{9,17},{17,25},{2,10},{10,18},{18,26},{... | collective-permute-start | bytes 786440 | tf_op jit(solution)/shard_map/ppermute | solution.py:14
  97.8 9.2 %collective-permute-start.13 = (bf16[128,1024]{1,0:T(8,128)(2,1)S(1)}, bf16[128,1024]{1,0:T(8,128)(2,1)S(1)}, u32[]{:S(2)}, u32[]{:S(2)}) collective-permute-start(bf16[128,1024]{1,0:T(8,128)(2,1)S(1)} %fusion.13), channel_id=1, source_target_pairs={{0,2},{2,4},{4,6},{1,3},{3,5},{5,7},{8,10},{10,12},{12,14},{9,11},... | collective-permute-start | bytes 786440 | tf_op jit(solution)/shard_map/ppermute | solution.py:14
  107.8 1.0 copy-start.2
  108.7 12.8 %copy-start = (bf16[256,2048]{1,0:T(8,128)(2,1)}, bf16[256,2048]{1,0:T(8,128)(2,1)S(1)}, u32[]{:S(2)}) copy-start(bf16[256,2048]{1,0:T(8,128)(2,1)S(1)} %fusion.39) | copy-start | bytes 3145732

commit v2 on v1

--- a/solution.py
+++ b/solution.py
@@ -5,13 +5,22 @@
 
 DB = 128
 BLOCKS = 2
-ORDER = 'rl'
+SKEW = 1
 
 
-def passed_along(shard, axis, by):
-    peers = lax.axis_size(axis)
-    pairs = [(i, i + by) for i in range(peers) if 0 <= i + by < peers]
-    return lax.ppermute(shard, axis, pairs)
+def passed_along(shard, moment, down, rows, cols):
+    pairs = []
+    for r in range(rows):
+        for c in range(cols):
+            if not 0 <= moment - SKEW * (r + c) < BLOCKS:
+                continue
+            if down and r + 1 < rows:
+                pairs.append((r * cols + c, (r + 1) * cols + c))
+            if not down and c + 1 < cols:
+                pairs.append((r * cols + c, r * cols + c + 1))
+    if not pairs:
+        return jnp.zeros_like(shard)
+    return lax.ppermute(shard, ("row", "col"), pairs)
 
 
 def on_device(green, background, wavelet, station_cell, fault_point, fault_owner, fault_row):
@@ -27,39 +36,30 @@
         own_source, wavelet.astype(jnp.float32), 0.0
     )
     height = stations // BLOCKS
-    total_fronts = row_count + col_count + BLOCKS - 2
+    total_fronts = SKEW * (row_count + col_count - 2) + BLOCKS
     down_in = jnp.zeros((height, half), jnp.bfloat16)
     right_in = jnp.zeros((height, half), jnp.bfloat16)
     field = jnp.zeros((stations, 2 * half), jnp.bfloat16)
+    inbox = {}
     for moment in range(total_fronts):
-        block = moment - row_place - col_place
+        block = moment - SKEW * (row_place + col_place)
         active = jnp.logical_and(block >= 0, block < BLOCKS)
         start = jnp.clip(block, 0, BLOCKS - 1) * height
         part = lax.dynamic_slice_in_dim(source, start, height, 0)
-        joined = jnp.concatenate([down_in, right_in], axis=1)
-        if ORDER == "one":
-            update = (jnp.dot(joined, matrix, preferred_element_type=jnp.float32) + part).astype(jnp.bfloat16)
-            lower, right = update[:, :half], update[:, half:]
-            right_next = passed_along(right, "col", 1)
-            down_next = passed_along(lower, "row", 1)
+        if moment < SKEW:
+            lower = part[:, :half].astype(jnp.bfloat16)
+            right = part[:, half:].astype(jnp.bfloat16)
         else:
-            def face(lo):
-                cols = slice(0, half) if lo else slice(half, 2 * half)
-                return (jnp.dot(joined, matrix[:, cols], preferred_element_type=jnp.float32) + part[:, cols]).astype(jnp.bfloat16)
-            if ORDER == "rl":
-                right = face(False)
-                right_next = passed_along(right, "col", 1)
-                lower = face(True)
-                down_next = passed_along(lower, "row", 1)
-            else:
-                lower = face(True)
-                down_next = passed_along(lower, "row", 1)
-                right = face(False)
-                right_next = passed_along(right, "col", 1)
-            update = jnp.concatenate([lower, right], axis=1)
+            down_in, right_in = inbox.pop(moment)
+            joined = jnp.concatenate([down_in, right_in], axis=1)
+            right = (jnp.dot(joined, matrix[:, half:], preferred_element_type=jnp.float32) + part[:, half:]).astype(jnp.bfloat16)
+            lower = (jnp.dot(joined, matrix[:, :half], preferred_element_type=jnp.float32) + part[:, :half]).astype(jnp.bfloat16)
+        right_next = passed_along(right, moment, False, row_count, col_count)
+        down_next = passed_along(lower, moment, True, row_count, col_count)
+        inbox[moment + SKEW] = (down_next, right_next)
+        update = jnp.concatenate([lower, right], axis=1)
         previous = lax.dynamic_slice_in_dim(field, start, height, 0)
         field = lax.dynamic_update_slice_in_dim(field, jnp.where(active, update, previous), start, 0)
-        down_in, right_in = down_next, right_next
     points = fault_point[0]
     owners = fault_owner[0, :, 0]
     targets = fault_row[0]

time: 122 us -> 91 us (0.75)
  the two profiles are of different devices: /device:TPU:0 before, /device:TPU:24 now
where the time goes in v2:
time: 91 us; the launch traced here: 90.6 us
  blocking collectives  24.3 us (27%)
  waiting for transfers between devices  23.8 us (26%)
  starting transfers between devices  17.7 us (19%)
  matrix products  16.7 us (18%)
  other arithmetic  4.5 us (5%)
  local copies, waits for them, and re-layouts  2.26 us (2%)
  between operations  1.23 us (1%)
    all_to_all x1, blocking collectives, on_device(): lax.all_to_all(message, 'col', split_axis=0, concat_axis=0, tiled=True)  24.3 us
    ppermute x14, waiting for transfers between devices, passed_along(): return lax.ppermute(shard, ('row', 'col'), pairs)  23.8 us
    ppermute x14, starting transfers between devices, passed_along(): return lax.ppermute(shard, ('row', 'col'), pairs)  17.7 us
    dot_general x7, matrix products, on_device(): jnp.dot(joined, matrix[:, half:], preferred_element_type=jnp.float32)  7.79 us
    dot_general x7, matrix products, on_device(): jnp.dot(joined, matrix[:, :half], preferred_element_type=jnp.float32)  7.59 us
    add x1, other arithmetic, on_device(): background[0, 0].astype(jnp.float32)  1.88 us
  transfers between devices with their start and end apart: 14, of which 3 were waited for; matrix products, arithmetic and copies ran while one was open for 11% of the time, Pallas kernels for 0%

profile of v2, /device:TPU:24, one launch (start us, length us, event | category | flops | bytes accessed | tf_op | source)
XLA Modules:
  0.0 90.6 jit_solution(16254448696686932495)
XLA Ops:
  0.7 0.7 broadcast_compare_fusion
  1.3 1.9 %convert_add_fusion = f32[256,2048]{1,0:T(8,128)S(1)} fusion(bf16[256,2048]{1,0:T(8,128)(2,1)} %param.9, bf16[1,1,256,2048]{3,2,1,0:T(8,128)(2,1)} %param.8, pred[256]{0:T(512)(128)(4,1)S(1)} %broadcast_compare_fusion), kind=kLoop, calls=%fused_computation | loop fusion | flops 2097152 | bytes 4194560 | tf_op jit(solution)/shard_map/add | solution.py:35
  3.5 0.8 fusion.69
  4.3 1.4 %collective-permute-start = (bf16[128,1024]{1,0:T(8,128)(2,1)}, bf16[128,1024]{1,0:T(8,128)(2,1)}, u32[]{:S(2)}, u32[]{:S(2)}) collective-permute-start(bf16[128,1024]{1,0:T(8,128)(2,1)} %get-tuple-element.5), channel_id=1, source_target_pairs={{0,8},{1,9}} | collective-permute-start | bytes 786440 | tf_op jit(solution)/shard_map/ppermute | solution.py:23
  6.8 1.0 %constant_dynamic-update-slice_fusion.1 = bf16[128,2048]{1,0:T(8,128)(2,1)S(1)} fusion(bf16[128,1024]{1,0:T(8,128)(2,1)} %collective-permute-done), kind=kLoop, calls=%fused_computation.67 | loop fusion | bytes 524288
  7.9 3.1 %fusion.14 = bf16[128,1024]{1,0:T(8,128)(2,1)S(1)} fusion(bf16[128,2048]{1,0:T(8,128)(2,1)S(1)} %constant_dynamic-update-slice_fusion, bf16[2048,2048]{1,0:T(8,128)(2,1)} %bitcast.36, f32[256,2048]{1,0:T(8,128)S(1)} %convert_add_fusion, s32[]{:T(128)S(6)} %select_n.102), kind=kOutput, calls=%fused_computation.29 | convolution fusion | flops 537133056 | bytes 5505028 | tf_op jit(solution)/shard_map/dot_general | solution.py:56
  11.0 0.8 collective-permute-start.2
  11.8 3.3 %fusion.17 = bf16[128,1024]{1,0:T(8,128)(2,1)S(1)} fusion(bf16[128,2048]{1,0:T(8,128)(2,1)S(1)} %constant_dynamic-update-slice_fusion, bf16[2048,2048]{1,0:T(8,128)(2,1)} %bitcast.37, f32[256,2048]{1,0:T(8,128)S(1)} %convert_add_fusion, s32[]{:T(128)S(6)} %select_n.102, s32[]{:T(128)S(6)} %add.141), kind=kOutput, calls=%fused_computation.30 | convolution fusion | flops 537133056 | bytes 5505032 | tf_op jit(solution)/shard_map/dot_general | solution.py:55
  15.1 0.7 collective-permute-start.3
  16.1 0.7 fusion.20
  16.8 1.3 %collective-permute-start.4 = (bf16[128,1024]{1,0:T(8,128)(2,1)S(1)}, bf16[128,1024]{1,0:T(8,128)(2,1)S(1)}, u32[]{:S(2)}, u32[]{:S(2)}) collective-permute-start(bf16[128,1024]{1,0:T(8,128)(2,1)S(1)} %fusion.20), channel_id=1, source_target_pairs={{2,10},{4,12},{8,16},{10,18},{16,24},{3,11},{5,13},{9,17},{11,19},... | collective-permute-start | bytes 786440 | tf_op jit(solution)/shard_map/ppermute | solution.py:23
  18.1 0.8 fusion.23
  18.9 0.7 collective-permute-start.5
  19.8 14.9 %collective-permute-done.4 = bf16[128,1024]{1,0:T(8,128)(2,1)S(1)} collective-permute-done((bf16[128,1024]{1,0:T(8,128)(2,1)S(1)}, bf16[128,1024]{1,0:T(8,128)(2,1)S(1)}, u32[]{:S(2)}, u32[]{:S(2)}) %collective-permute-start.4) | collective-permute-done | bytes 262176 | tf_op jit(solution)/shard_map/ppermute | solution.py:23
  34.8 0.7 fusion.26
  35.5 1.3 %collective-permute-start.6 = (bf16[128,1024]{1,0:T(8,128)(2,1)S(1)}, bf16[128,1024]{1,0:T(8,128)(2,1)S(1)}, u32[]{:S(2)}, u32[]{:S(2)}) collective-permute-start(bf16[128,1024]{1,0:T(8,128)(2,1)S(1)} %fusion.26), channel_id=1, source_target_pairs={{4,12},{6,14},{10,18},{12,20},{16,24},{18,26},{5,13},{7,15},{11,19... | collective-permute-start | bytes 786440 | tf_op jit(solution)/shard_map/ppermute | solution.py:23
  36.8 0.7 fusion.29
  37.6 1.3 %collective-permute-start.7 = (bf16[128,1024]{1,0:T(8,128)(2,1)S(1)}, bf16[128,1024]{1,0:T(8,128)(2,1)S(1)}, u32[]{:S(2)}, u32[]{:S(2)}) collective-permute-start(bf16[128,1024]{1,0:T(8,128)(2,1)S(1)} %fusion.29), channel_id=1, source_target_pairs={{4,6},{10,12},{12,14},{16,18},{18,20},{24,26},{5,7},{11,13},{13,15... | collective-permute-start | bytes 786440 | tf_op jit(solution)/shard_map/ppermute | solution.py:23
  39.1 5.2 %collective-permute-done.6 = bf16[128,1024]{1,0:T(8,128)(2,1)S(1)} collective-permute-done((bf16[128,1024]{1,0:T(8,128)(2,1)S(1)}, bf16[128,1024]{1,0:T(8,128)(2,1)S(1)}, u32[]{:S(2)}, u32[]{:S(2)}) %collective-permute-start.6) | collective-permute-done | bytes 262176 | tf_op jit(solution)/shard_map/ppermute | solution.py:23
  44.3 0.7 fusion.32
  45.8 0.8 fusion.35
  46.5 6.3 %collective-permute-start.9 = (bf16[128,1024]{1,0:T(8,128)(2,1)S(1)}, bf16[128,1024]{1,0:T(8,128)(2,1)S(1)}, u32[]{:S(2)}, u32[]{:S(2)}) collective-permute-start(bf16[128,1024]{1,0:T(8,128)(2,1)S(1)} %fusion.35), channel_id=1, source_target_pairs={{12,14},{18,20},{20,22},{24,26},{26,28},{13,15},{19,21},{21,23},{2... | collective-permute-start | bytes 786440 | tf_op jit(solution)/shard_map/ppermute | solution.py:23
  53.0 3.6 %collective-permute-done.9 = bf16[128,1024]{1,0:T(8,128)(2,1)S(1)} collective-permute-done((bf16[128,1024]{1,0:T(8,128)(2,1)S(1)}, bf16[128,1024]{1,0:T(8,128)(2,1)S(1)}, u32[]{:S(2)}, u32[]{:S(2)}) %collective-permute-start.9) | collective-permute-done | bytes 262176 | tf_op jit(solution)/shard_map/ppermute | solution.py:23
  56.7 0.7 fusion.38
  58.1 0.8 fusion.41
  58.9 0.7 collective-permute-start.11
  59.8 0.7 fusion.44
  61.3 0.8 fusion.47
  63.0 0.8 fusion.53
  63.8 0.7 fusion.50
  65.3 24.3 %all_to_all.5 = bf16[4,8,384]{2,1,0:T(8,128)(2,1)S(1)} all-to-all(bf16[4,8,384]{2,1,0:T(8,128)(2,1)S(1)} %maximum_bitcast_fusion), channel_id=1, replica_groups=mesh['row'=4,'col'=4,'batch'=2] {'col'}, dimensions={0} | all-to-all | bytes 49152 | tf_op jit(solution)/shard_map/all_to_all | solution.py:80
  89.7 0.8 convolution_bitcast_fusion
  (62 shorter events, 6.3 us)
Async XLA Ops:
  0.6 5.7 %copy-start.3 = (s32[1,16]{1,0:T(1,128)S(1)}, s32[1,16]{1,0:T(1,128)}, u32[]{:S(2)}) copy-start(s32[1,16]{1,0:T(1,128)} %param.13) | copy-start | bytes 196
  0.6 5.7 %copy-start.1 = (s32[1,16,1]{1,2,0:T(1,128)S(1)}, s32[1,16,1]{1,2,0:T(1,128)}, u32[]{:S(2)}) copy-start(s32[1,16,1]{1,2,0:T(1,128)} %param.12) | copy-start | bytes 196
  4.3 2.5 %collective-permute-start = (bf16[128,1024]{1,0:T(8,128)(2,1)}, bf16[128,1024]{1,0:T(8,128)(2,1)}, u32[]{:S(2)}, u32[]{:S(2)}) collective-permute-start(bf16[128,1024]{1,0:T(8,128)(2,1)} %get-tuple-element.5), channel_id=1, source_target_pairs={{0,8},{1,9}} | collective-permute-start | bytes 786440 | tf_op jit(solution)/shard_map/ppermute | solution.py:23
  5.7 2.2 %collective-permute-start.1 = (bf16[128,1024]{1,0:T(8,128)(2,1)}, bf16[128,1024]{1,0:T(8,128)(2,1)S(1)}, u32[]{:S(2)}, u32[]{:S(2)}) collective-permute-start(bf16[128,1024]{1,0:T(8,128)(2,1)} %get-tuple-element.4), channel_id=1, source_target_pairs={{0,2},{1,3}} | collective-permute-start | bytes 786440 | tf_op jit(solution)/shard_map/ppermute | solution.py:23
  7.8 8.2 %slice-start = ((s8[8388608]{0:T(1024)(128)(4,1)}), s8[4194304]{0:T(1024)(128)(4,1)S(1)}, s32[]{:S(2)}) async-start(s8[8388608]{0:T(1024)(128)(4,1)} %bitcast.38), calls=%async_computation.1 | async-start | bytes 8388608
  11.0 5.1 %slice-start.1 = ((s8[8388608]{0:T(1024)(128)(4,1)}), s8[4194304]{0:T(1024)(128)(4,1)S(1)}, s32[]{:S(2)}) async-start(s8[8388608]{0:T(1024)(128)(4,1)} %bitcast.38), calls=%async_computation.2 | async-start | bytes 8388608
  11.0 5.0 %collective-permute-start.2 = (bf16[128,1024]{1,0:T(8,128)(2,1)S(1)}, bf16[128,1024]{1,0:T(8,128)(2,1)S(1)}, u32[]{:S(2)}, u32[]{:S(2)}) collective-permute-start(bf16[128,1024]{1,0:T(8,128)(2,1)S(1)} %fusion.14), channel_id=1, source_target_pairs={{0,8},{2,10},{8,16},{1,9},{3,11},{9,17}} | collective-permute-start | bytes 786440 | tf_op jit(solution)/shard_map/ppermute | solution.py:23
  15.1 0.9 %collective-permute-start.3 = (bf16[128,1024]{1,0:T(8,128)(2,1)S(1)}, bf16[128,1024]{1,0:T(8,128)(2,1)S(1)}, u32[]{:S(2)}, u32[]{:S(2)}) collective-permute-start(bf16[128,1024]{1,0:T(8,128)(2,1)S(1)} %fusion.17), channel_id=1, source_target_pairs={{0,2},{2,4},{8,10},{1,3},{3,5},{9,11}} | collective-permute-start | bytes 786440 | tf_op jit(solution)/shard_map/ppermute | solution.py:23
  16.8 17.9 %collective-permute-start.4 = (bf16[128,1024]{1,0:T(8,128)(2,1)S(1)}, bf16[128,1024]{1,0:T(8,128)(2,1)S(1)}, u32[]{:S(2)}, u32[]{:S(2)}) collective-permute-start(bf16[128,1024]{1,0:T(8,128)(2,1)S(1)} %fusion.20), channel_id=1, source_target_pairs={{2,10},{4,12},{8,16},{10,18},{16,24},{3,11},{5,13},{9,17},{11,19},... | collective-permute-start | bytes 786440 | tf_op jit(solution)/shard_map/ppermute | solution.py:23
  18.9 15.8 %collective-permute-start.5 = (bf16[128,1024]{1,0:T(8,128)(2,1)S(1)}, bf16[128,1024]{1,0:T(8,128)(2,1)S(1)}, u32[]{:S(2)}, u32[]{:S(2)}) collective-permute-start(bf16[128,1024]{1,0:T(8,128)(2,1)S(1)} %fusion.23), channel_id=1, source_target_pairs={{2,4},{4,6},{8,10},{10,12},{16,18},{3,5},{5,7},{9,11},{11,13},{17,... | collective-permute-start | bytes 786440 | tf_op jit(solution)/shard_map/ppermute | solution.py:23
  35.5 8.8 %collective-permute-start.6 = (bf16[128,1024]{1,0:T(8,128)(2,1)S(1)}, bf16[128,1024]{1,0:T(8,128)(2,1)S(1)}, u32[]{:S(2)}, u32[]{:S(2)}) collective-permute-start(bf16[128,1024]{1,0:T(8,128)(2,1)S(1)} %fusion.26), channel_id=1, source_target_pairs={{4,12},{6,14},{10,18},{12,20},{16,24},{18,26},{5,13},{7,15},{11,19... | collective-permute-start | bytes 786440 | tf_op jit(solution)/shard_map/ppermute | solution.py:23
  37.6 6.7 %collective-permute-start.7 = (bf16[128,1024]{1,0:T(8,128)(2,1)S(1)}, bf16[128,1024]{1,0:T(8,128)(2,1)S(1)}, u32[]{:S(2)}, u32[]{:S(2)}) collective-permute-start(bf16[128,1024]{1,0:T(8,128)(2,1)S(1)} %fusion.29), channel_id=1, source_target_pairs={{4,6},{10,12},{12,14},{16,18},{18,20},{24,26},{5,7},{11,13},{13,15... | collective-permute-start | bytes 786440 | tf_op jit(solution)/shard_map/ppermute | solution.py:23
  45.1 7.9 %collective-permute-start.8 = (bf16[128,1024]{1,0:T(8,128)(2,1)S(1)}, bf16[128,1024]{1,0:T(8,128)(2,1)S(1)}, u32[]{:S(2)}, u32[]{:S(2)}) collective-permute-start(bf16[128,1024]{1,0:T(8,128)(2,1)S(1)} %fusion.32), channel_id=1, source_target_pairs={{6,14},{12,20},{14,22},{18,26},{20,28},{7,15},{13,21},{15,23},{19,... | collective-permute-start | bytes 786440 | tf_op jit(solution)/shard_map/ppermute | solution.py:23
  46.5 10.1 %collective-permute-start.9 = (bf16[128,1024]{1,0:T(8,128)(2,1)S(1)}, bf16[128,1024]{1,0:T(8,128)(2,1)S(1)}, u32[]{:S(2)}, u32[]{:S(2)}) collective-permute-start(bf16[128,1024]{1,0:T(8,128)(2,1)S(1)} %fusion.35), channel_id=1, source_target_pairs={{12,14},{18,20},{20,22},{24,26},{26,28},{13,15},{19,21},{21,23},{2... | collective-permute-start | bytes 786440 | tf_op jit(solution)/shard_map/ppermute | solution.py:23
  57.4 2.3 %collective-permute-start.10 = (bf16[128,1024]{1,0:T(8,128)(2,1)S(1)}, bf16[128,1024]{1,0:T(8,128)(2,1)S(1)}, u32[]{:S(2)}, u32[]{:S(2)}) collective-permute-start(bf16[128,1024]{1,0:T(8,128)(2,1)S(1)} %fusion.38), channel_id=1, source_target_pairs={{14,22},{20,28},{22,30},{15,23},{21,29},{23,31}} | collective-permute-start | bytes 786440 | tf_op jit(solution)/shard_map/ppermute | solution.py:23
  58.9 0.9 %collective-permute-start.11 = (bf16[128,1024]{1,0:T(8,128)(2,1)S(1)}, bf16[128,1024]{1,0:T(8,128)(2,1)S(1)}, u32[]{:S(2)}, u32[]{:S(2)}) collective-permute-start(bf16[128,1024]{1,0:T(8,128)(2,1)S(1)} %fusion.41), channel_id=1, source_target_pairs={{20,22},{26,28},{28,30},{21,23},{27,29},{29,31}} | collective-permute-start | bytes 786440 | tf_op jit(solution)/shard_map/ppermute | solution.py:23
  60.6 2.3 %collective-permute-start.12 = (bf16[128,1024]{1,0:T(8,128)(2,1)S(1)}, bf16[128,1024]{1,0:T(8,128)(2,1)S(1)}, u32[]{:S(2)}, u32[]{:S(2)}) collective-permute-start(bf16[128,1024]{1,0:T(8,128)(2,1)S(1)} %fusion.44), channel_id=1, source_target_pairs={{22,30},{23,31}} | collective-permute-start | bytes 786440 | tf_op jit(solution)/shard_map/ppermute | solution.py:23
  62.0 0.9 %collective-permute-start.13 = (bf16[128,1024]{1,0:T(8,128)(2,1)S(1)}, bf16[128,1024]{1,0:T(8,128)(2,1)S(1)}, u32[]{:S(2)}, u32[]{:S(2)}) collective-permute-start(bf16[128,1024]{1,0:T(8,128)(2,1)S(1)} %fusion.47), channel_id=1, source_target_pairs={{28,30},{29,31}} | collective-permute-start | bytes 786440 | tf_op jit(solution)/shard_map/ppermute | solution.py:23
  63.7 1.0 %copy-start.2 = (s32[1,16]{1,0:T(1,128)S(1)}, s32[1,16]{1,0:T(1,128)}, u32[]{:S(2)}) copy-start(s32[1,16]{1,0:T(1,128)} %param.11) | copy-start | bytes 196
  64.7 25.9 %copy-start = (bf16[256,2048]{1,0:T(8,128)(2,1)}, bf16[256,2048]{1,0:T(8,128)(2,1)S(1)}, u32[]{:S(2)}) copy-start(bf16[256,2048]{1,0:T(8,128)(2,1)S(1)} %fusion.62) | copy-start | bytes 3145732

commit v3 on v2

--- a/solution.py
+++ b/solution.py
@@ -49,6 +49,13 @@
         if moment < SKEW:
             lower = part[:, :half].astype(jnp.bfloat16)
             right = part[:, half:].astype(jnp.bfloat16)
+        elif moment == SKEW and SKEW == 1:
+            down_in, right_in = inbox.pop(moment)
+            arrived = down_in + right_in
+            rows_from = jnp.where(row_place == 0, half, 0)
+            rows = lax.dynamic_slice_in_dim(matrix, rows_from, half, 0)
+            right = (jnp.dot(arrived, rows[:, half:], preferred_element_type=jnp.float32) + part[:, half:]).astype(jnp.bfloat16)
+            lower = (jnp.dot(arrived, rows[:, :half], preferred_element_type=jnp.float32) + part[:, :half]).astype(jnp.bfloat16)
         else:
             down_in, right_in = inbox.pop(moment)
             joined = jnp.concatenate([down_in, right_in], axis=1)

time: 91 us -> 90.3 us (level)
  waiting for transfers between devices: 23.8 us -> 18.7 us
  local copies, waits for them, and re-layouts: 2.26 us -> 5.92 us
    ppermute x14, waiting for transfers between devices: 23.8 us -> 18.7 us  [passed_along(): return lax.ppermute(shard, ('row', 'col'), pairs)]
    dynamic_slice x0 -> x1, local copies, waits for them, and re-layouts: none -> 4.73 us  [on_device(): rows = lax.dynamic_slice_in_dim(matrix, rows_from, half, 0)]
    dot_general x0 -> x2, matrix products: none -> 4.57 us  [the longest x1 2.35 us: on_device(): jnp.dot(arrived, rows[:, :half], preferred_element_type=jnp.float32)]
    dot_general x7 -> x6, matrix products: 7.79 us -> 4.45 us  [on_device(): jnp.dot(joined, matrix[:, half:], preferred_element_type=jnp.float32)]
    unnamed x19 -> x18, local copies, waits for them, and re-layouts: 1.12 us -> 0.15 us
    dot_general x7 -> x6, matrix products: 7.59 us -> 6.79 us  [on_device(): jnp.dot(joined, matrix[:, :half], preferred_element_type=jnp.float32)]
  transfers between devices with their start and end apart: 14 -> 14, of which waited for: 3 -> 3; matrix products, arithmetic and copies ran while one was open for 11% -> 14% of each run, Pallas kernels for 0% -> 0%
where the time goes in v3:
time: 90.3 us; the launch traced here: 89.9 us
  blocking collectives  24.4 us (27%)
  waiting for transfers between devices  18.7 us (21%)
  starting transfers between devices  18.1 us (20%)
  matrix products  17.1 us (19%)
  local copies, waits for them, and re-layouts  5.92 us (7%)
  other arithmetic  4.48 us (5%)
  between operations  1.2 us (1%)
    all_to_all x1, blocking collectives, on_device(): lax.all_to_all(message, 'col', split_axis=0, concat_axis=0, tiled=True)  24.4 us
    ppermute x14, waiting for transfers between devices, passed_along(): return lax.ppermute(shard, ('row', 'col'), pairs)  18.7 us
    ppermute x14, starting transfers between devices, passed_along(): return lax.ppermute(shard, ('row', 'col'), pairs)  18.1 us
    dot_general x6, matrix products, on_device(): jnp.dot(joined, matrix[:, :half], preferred_element_type=jnp.float32)  6.79 us
    dynamic_slice x1, local copies, waits for them, and re-layouts, on_device(): rows = lax.dynamic_slice_in_dim(matrix, rows_from, half, 0)  4.73 us
    dot_general x6, matrix products, on_device(): jnp.dot(joined, matrix[:, half:], preferred_element_type=jnp.float32)  4.45 us
    dot_general x1, matrix products, on_device(): jnp.dot(arrived, rows[:, :half], preferred_element_type=jnp.float32)  2.35 us
    dot_general x1, matrix products, on_device(): jnp.dot(arrived, rows[:, half:], preferred_element_type=jnp.float32)  2.22 us
  transfers between devices with their start and end apart: 14, of which 3 were waited for; matrix products, arithmetic and copies ran while one was open for 14% of the time, Pallas kernels for 0%

profile of v3, /device:TPU:24, one launch (start us, length us, event | category | flops | bytes accessed | tf_op | source)
XLA Modules:
  0.0 89.9 jit_solution(17727900519216424112)
XLA Ops:
  0.7 0.7 broadcast_compare_fusion
  1.4 1.9 %convert_add_fusion = f32[256,2048]{1,0:T(8,128)S(1)} fusion(bf16[256,2048]{1,0:T(8,128)(2,1)} %param.9, bf16[1,1,256,2048]{3,2,1,0:T(8,128)(2,1)} %param.8, pred[256]{0:T(512)(128)(4,1)S(1)} %broadcast_compare_fusion), kind=kLoop, calls=%fused_computation.5 | loop fusion | flops 2097152 | bytes 4194560 | tf_op jit(solution)/shard_map/add | solution.py:35
  3.5 0.7 fusion.127
  4.2 1.4 %collective-permute-start = (bf16[128,1024]{1,0:T(8,128)(2,1)}, bf16[128,1024]{1,0:T(8,128)(2,1)}, u32[]{:S(2)}, u32[]{:S(2)}) collective-permute-start(bf16[128,1024]{1,0:T(8,128)(2,1)} %get-tuple-element.5), channel_id=1, source_target_pairs={{0,8},{1,9}} | collective-permute-start | bytes 786440 | tf_op jit(solution)/shard_map/ppermute | solution.py:23
  5.6 1.4 %collective-permute-start.1 = (bf16[128,1024]{1,0:T(8,128)(2,1)S(1)}, bf16[128,1024]{1,0:T(8,128)(2,1)}, u32[]{:S(2)}, u32[]{:S(2)}) collective-permute-start(bf16[128,1024]{1,0:T(8,128)(2,1)S(1)} %get-tuple-element.4), channel_id=1, source_target_pairs={{0,2},{1,3}} | collective-permute-start | bytes 786440 | tf_op jit(solution)/shard_map/ppermute | solution.py:23
  7.3 4.7 %dynamic-slice_bitcast_fusion = bf16[1024,2048]{1,0:T(8,128)(2,1)} fusion(bf16[1,1,2048,2048]{3,2,1,0:T(8,128)(2,1)} %param.7, s32[]{:T(128)S(6)} %select_n.107), kind=kLoop, calls=%fused_computation | loop fusion | bytes 8388612 | tf_op jit(solution)/shard_map/dynamic_slice | solution.py:56
  12.2 2.4 %fusion.109 = bf16[128,1024]{1,0:T(8,128)(2,1)S(1)} fusion(bf16[1024,2048]{1,0:T(8,128)(2,1)} %dynamic-slice_bitcast_fusion, f32[256,2048]{1,0:T(8,128)S(1)} %convert_add_fusion, s32[]{:T(128)S(6)} %select_n.108, bf16[128,1024]{1,0:T(8,128)(2,1)} %collective-permute-done, bf16[128,1024]{1,0:T(8,128)(2,1)} %collective-permute-done.1), kind=kOutput, calls=%fused_computation.57 | convolution fusion | flops 268828672 | bytes 3407876 | tf_op jit(solution)/shard_map/dot_general | solution.py:58
  14.6 0.7 collective-permute-start.2
  15.2 2.2 %fusion.106 = bf16[128,1024]{1,0:T(8,128)(2,1)S(1)} fusion(bf16[1024,2048]{1,0:T(8,128)(2,1)} %dynamic-slice_bitcast_fusion, f32[256,2048]{1,0:T(8,128)S(1)} %convert_add_fusion, s32[]{:T(128)S(6)} %select_n.108, s32[]{:T(128)S(6)} %add.146, bf16[128,1024]{1,0:T(8,128)(2,1)} %collective-permute-done, bf16[128,1024]{1,0:T(8,128)(2,1)} %collective-permute-done.1), kind=kOutput, calls=%fused_computation.56 | convolution fusion | flops 268828672 | bytes 3407880 | tf_op jit(solution)/shard_map/dot_general | solution.py:57
  17.5 0.7 collective-permute-start.3
  18.4 3.1 %fusion.103 = bf16[128,1024]{1,0:T(8,128)(2,1)S(1)} fusion(bf16[128,2048]{1,0:T(8,128)(2,1)S(1)} %constant_dynamic-update-slice_fusion, bf16[2048,2048]{1,0:T(8,128)(2,1)} %bitcast.31, f32[256,2048]{1,0:T(8,128)S(1)} %convert_add_fusion, s32[]{:T(128)S(6)} %select_n.111), kind=kOutput, calls=%fused_computation.55 | convolution fusion | flops 537133056 | bytes 5505028 | tf_op jit(solution)/shard_map/dot_general | solution.py:63
  21.5 1.3 %collective-permute-start.4 = (bf16[128,1024]{1,0:T(8,128)(2,1)S(1)}, bf16[128,1024]{1,0:T(8,128)(2,1)S(1)}, u32[]{:S(2)}, u32[]{:S(2)}) collective-permute-start(bf16[128,1024]{1,0:T(8,128)(2,1)S(1)} %fusion.103), channel_id=1, source_target_pairs={{2,10},{4,12},{8,16},{10,18},{16,24},{3,11},{5,13},{9,17},{11,19},... | collective-permute-start | bytes 786440 | tf_op jit(solution)/shard_map/ppermute | solution.py:23
  22.9 0.7 fusion.85
  23.6 0.7 collective-permute-start.5
  24.5 10.3 %collective-permute-done.4 = bf16[128,1024]{1,0:T(8,128)(2,1)S(1)} collective-permute-done((bf16[128,1024]{1,0:T(8,128)(2,1)S(1)}, bf16[128,1024]{1,0:T(8,128)(2,1)S(1)}, u32[]{:S(2)}, u32[]{:S(2)}) %collective-permute-start.4) | collective-permute-done | bytes 262176 | tf_op jit(solution)/shard_map/ppermute | solution.py:23
  34.9 0.7 fusion.100
  35.6 1.3 %collective-permute-start.6 = (bf16[128,1024]{1,0:T(8,128)(2,1)S(1)}, bf16[128,1024]{1,0:T(8,128)(2,1)S(1)}, u32[]{:S(2)}, u32[]{:S(2)}) collective-permute-start(bf16[128,1024]{1,0:T(8,128)(2,1)S(1)} %fusion.100), channel_id=1, source_target_pairs={{4,12},{6,14},{10,18},{12,20},{16,24},{18,26},{5,13},{7,15},{11,19... | collective-permute-start | bytes 786440 | tf_op jit(solution)/shard_map/ppermute | solution.py:23
  36.9 0.7 fusion.82
  37.6 1.3 %collective-permute-start.7 = (bf16[128,1024]{1,0:T(8,128)(2,1)S(1)}, bf16[128,1024]{1,0:T(8,128)(2,1)S(1)}, u32[]{:S(2)}, u32[]{:S(2)}) collective-permute-start(bf16[128,1024]{1,0:T(8,128)(2,1)S(1)} %fusion.82), channel_id=1, source_target_pairs={{4,6},{10,12},{12,14},{16,18},{18,20},{24,26},{5,7},{11,13},{13,15... | collective-permute-start | bytes 786440 | tf_op jit(solution)/shard_map/ppermute | solution.py:23
  39.1 4.7 %collective-permute-done.6 = bf16[128,1024]{1,0:T(8,128)(2,1)S(1)} collective-permute-done((bf16[128,1024]{1,0:T(8,128)(2,1)S(1)}, bf16[128,1024]{1,0:T(8,128)(2,1)S(1)}, u32[]{:S(2)}, u32[]{:S(2)}) %collective-permute-start.6) | collective-permute-done | bytes 262176 | tf_op jit(solution)/shard_map/ppermute | solution.py:23
  43.9 0.7 fusion.97
  45.4 0.7 fusion.79
  46.1 6.0 %collective-permute-start.9 = (bf16[128,1024]{1,0:T(8,128)(2,1)S(1)}, bf16[128,1024]{1,0:T(8,128)(2,1)S(1)}, u32[]{:S(2)}, u32[]{:S(2)}) collective-permute-start(bf16[128,1024]{1,0:T(8,128)(2,1)S(1)} %fusion.79), channel_id=1, source_target_pairs={{12,14},{18,20},{20,22},{24,26},{26,28},{13,15},{19,21},{21,23},{2... | collective-permute-start | bytes 786440 | tf_op jit(solution)/shard_map/ppermute | solution.py:23
  52.4 3.6 %collective-permute-done.9 = bf16[128,1024]{1,0:T(8,128)(2,1)S(1)} collective-permute-done((bf16[128,1024]{1,0:T(8,128)(2,1)S(1)}, bf16[128,1024]{1,0:T(8,128)(2,1)S(1)}, u32[]{:S(2)}, u32[]{:S(2)}) %collective-permute-start.9) | collective-permute-done | bytes 262176 | tf_op jit(solution)/shard_map/ppermute | solution.py:23
  56.0 0.7 fusion.94
  57.5 0.7 fusion.76
  59.1 0.7 fusion.91
  60.6 0.7 fusion.73
  62.3 0.7 fusion.70
  63.0 0.7 fusion.88
  64.6 24.4 %all_to_all.5 = bf16[4,8,384]{2,1,0:T(8,128)(2,1)S(1)} all-to-all(bf16[4,8,384]{2,1,0:T(8,128)(2,1)S(1)} %maximum_bitcast_fusion), channel_id=1, replica_groups=mesh['row'=4,'col'=4,'batch'=2] {'col'}, dimensions={0} | all-to-all | bytes 49152 | tf_op jit(solution)/shard_map/all_to_all | solution.py:87
  89.1 0.8 convolution_bitcast_fusion
  (61 shorter events, 6.3 us)
Async XLA Ops:
  0.6 6.3 %copy-start.3 = (s32[1,16]{1,0:T(1,128)S(1)}, s32[1,16]{1,0:T(1,128)}, u32[]{:S(2)}) copy-start(s32[1,16]{1,0:T(1,128)} %param.13) | copy-start | bytes 196
  0.6 6.3 %copy-start.1 = (s32[1,16,1]{1,2,0:T(1,128)S(1)}, s32[1,16,1]{1,2,0:T(1,128)}, u32[]{:S(2)}) copy-start(s32[1,16,1]{1,2,0:T(1,128)} %param.12) | copy-start | bytes 196
  4.2 7.9 %collective-permute-start = (bf16[128,1024]{1,0:T(8,128)(2,1)}, bf16[128,1024]{1,0:T(8,128)(2,1)}, u32[]{:S(2)}, u32[]{:S(2)}) collective-permute-start(bf16[128,1024]{1,0:T(8,128)(2,1)} %get-tuple-element.5), channel_id=1, source_target_pairs={{0,8},{1,9}} | collective-permute-start | bytes 786440 | tf_op jit(solution)/shard_map/ppermute | solution.py:23
  5.6 6.6 %collective-permute-start.1 = (bf16[128,1024]{1,0:T(8,128)(2,1)S(1)}, bf16[128,1024]{1,0:T(8,128)(2,1)}, u32[]{:S(2)}, u32[]{:S(2)}) collective-permute-start(bf16[128,1024]{1,0:T(8,128)(2,1)S(1)} %get-tuple-element.4), channel_id=1, source_target_pairs={{0,2},{1,3}} | collective-permute-start | bytes 786440 | tf_op jit(solution)/shard_map/ppermute | solution.py:23
  12.2 10.6 %slice-start = ((s8[8388608]{0:T(1024)(128)(4,1)}), s8[4194304]{0:T(1024)(128)(4,1)S(1)}, s32[]{:S(2)}) async-start(s8[8388608]{0:T(1024)(128)(4,1)} %bitcast.32), calls=%async_computation.1 | async-start | bytes 8388608
  14.6 3.8 %collective-permute-start.2 = (bf16[128,1024]{1,0:T(8,128)(2,1)S(1)}, bf16[128,1024]{1,0:T(8,128)(2,1)S(1)}, u32[]{:S(2)}, u32[]{:S(2)}) collective-permute-start(bf16[128,1024]{1,0:T(8,128)(2,1)S(1)} %fusion.109), channel_id=1, source_target_pairs={{0,8},{2,10},{8,16},{1,9},{3,11},{9,17}} | collective-permute-start | bytes 786440 | tf_op jit(solution)/shard_map/ppermute | solution.py:23
  17.5 0.9 %collective-permute-start.3 = (bf16[128,1024]{1,0:T(8,128)(2,1)S(1)}, bf16[128,1024]{1,0:T(8,128)(2,1)S(1)}, u32[]{:S(2)}, u32[]{:S(2)}) collective-permute-start(bf16[128,1024]{1,0:T(8,128)(2,1)S(1)} %fusion.106), channel_id=1, source_target_pairs={{0,2},{2,4},{8,10},{1,3},{3,5},{9,11}} | collective-permute-start | bytes 786440 | tf_op jit(solution)/shard_map/ppermute | solution.py:23
  18.2 4.7 %slice-start.1 = ((s8[8388608]{0:T(1024)(128)(4,1)}), s8[4194304]{0:T(1024)(128)(4,1)S(1)}, s32[]{:S(2)}) async-start(s8[8388608]{0:T(1024)(128)(4,1)} %bitcast.32), calls=%async_computation.2 | async-start | bytes 8388608
  21.5 13.3 %collective-permute-start.4 = (bf16[128,1024]{1,0:T(8,128)(2,1)S(1)}, bf16[128,1024]{1,0:T(8,128)(2,1)S(1)}, u32[]{:S(2)}, u32[]{:S(2)}) collective-permute-start(bf16[128,1024]{1,0:T(8,128)(2,1)S(1)} %fusion.103), channel_id=1, source_target_pairs={{2,10},{4,12},{8,16},{10,18},{16,24},{3,11},{5,13},{9,17},{11,19},... | collective-permute-start | bytes 786440 | tf_op jit(solution)/shard_map/ppermute | solution.py:23
  23.6 11.2 %collective-permute-start.5 = (bf16[128,1024]{1,0:T(8,128)(2,1)S(1)}, bf16[128,1024]{1,0:T(8,128)(2,1)S(1)}, u32[]{:S(2)}, u32[]{:S(2)}) collective-permute-start(bf16[128,1024]{1,0:T(8,128)(2,1)S(1)} %fusion.85), channel_id=1, source_target_pairs={{2,4},{4,6},{8,10},{10,12},{16,18},{3,5},{5,7},{9,11},{11,13},{17,... | collective-permute-start | bytes 786440 | tf_op jit(solution)/shard_map/ppermute | solution.py:23
  35.6 8.3 %collective-permute-start.6 = (bf16[128,1024]{1,0:T(8,128)(2,1)S(1)}, bf16[128,1024]{1,0:T(8,128)(2,1)S(1)}, u32[]{:S(2)}, u32[]{:S(2)}) collective-permute-start(bf16[128,1024]{1,0:T(8,128)(2,1)S(1)} %fusion.100), channel_id=1, source_target_pairs={{4,12},{6,14},{10,18},{12,20},{16,24},{18,26},{5,13},{7,15},{11,19... | collective-permute-start | bytes 786440 | tf_op jit(solution)/shard_map/ppermute | solution.py:23
  37.6 6.2 %collective-permute-start.7 = (bf16[128,1024]{1,0:T(8,128)(2,1)S(1)}, bf16[128,1024]{1,0:T(8,128)(2,1)S(1)}, u32[]{:S(2)}, u32[]{:S(2)}) collective-permute-start(bf16[128,1024]{1,0:T(8,128)(2,1)S(1)} %fusion.82), channel_id=1, source_target_pairs={{4,6},{10,12},{12,14},{16,18},{18,20},{24,26},{5,7},{11,13},{13,15... | collective-permute-start | bytes 786440 | tf_op jit(solution)/shard_map/ppermute | solution.py:23
  44.7 7.7 %collective-permute-start.8 = (bf16[128,1024]{1,0:T(8,128)(2,1)S(1)}, bf16[128,1024]{1,0:T(8,128)(2,1)S(1)}, u32[]{:S(2)}, u32[]{:S(2)}) collective-permute-start(bf16[128,1024]{1,0:T(8,128)(2,1)S(1)} %fusion.97), channel_id=1, source_target_pairs={{6,14},{12,20},{14,22},{18,26},{20,28},{7,15},{13,21},{15,23},{19,... | collective-permute-start | bytes 786440 | tf_op jit(solution)/shard_map/ppermute | solution.py:23
  46.1 9.9 %collective-permute-start.9 = (bf16[128,1024]{1,0:T(8,128)(2,1)S(1)}, bf16[128,1024]{1,0:T(8,128)(2,1)S(1)}, u32[]{:S(2)}, u32[]{:S(2)}) collective-permute-start(bf16[128,1024]{1,0:T(8,128)(2,1)S(1)} %fusion.79), channel_id=1, source_target_pairs={{12,14},{18,20},{20,22},{24,26},{26,28},{13,15},{19,21},{21,23},{2... | collective-permute-start | bytes 786440 | tf_op jit(solution)/shard_map/ppermute | solution.py:23
  56.8 2.3 %collective-permute-start.10 = (bf16[128,1024]{1,0:T(8,128)(2,1)S(1)}, bf16[128,1024]{1,0:T(8,128)(2,1)S(1)}, u32[]{:S(2)}, u32[]{:S(2)}) collective-permute-start(bf16[128,1024]{1,0:T(8,128)(2,1)S(1)} %fusion.94), channel_id=1, source_target_pairs={{14,22},{20,28},{22,30},{15,23},{21,29},{23,31}} | collective-permute-start | bytes 786440 | tf_op jit(solution)/shard_map/ppermute | solution.py:23
  58.2 0.9 %collective-permute-start.11 = (bf16[128,1024]{1,0:T(8,128)(2,1)S(1)}, bf16[128,1024]{1,0:T(8,128)(2,1)S(1)}, u32[]{:S(2)}, u32[]{:S(2)}) collective-permute-start(bf16[128,1024]{1,0:T(8,128)(2,1)S(1)} %fusion.76), channel_id=1, source_target_pairs={{20,22},{26,28},{28,30},{21,23},{27,29},{29,31}} | collective-permute-start | bytes 786440 | tf_op jit(solution)/shard_map/ppermute | solution.py:23
  59.9 2.3 %collective-permute-start.12 = (bf16[128,1024]{1,0:T(8,128)(2,1)S(1)}, bf16[128,1024]{1,0:T(8,128)(2,1)S(1)}, u32[]{:S(2)}, u32[]{:S(2)}) collective-permute-start(bf16[128,1024]{1,0:T(8,128)(2,1)S(1)} %fusion.91), channel_id=1, source_target_pairs={{22,30},{23,31}} | collective-permute-start | bytes 786440 | tf_op jit(solution)/shard_map/ppermute | solution.py:23
  61.3 0.9 %collective-permute-start.13 = (bf16[128,1024]{1,0:T(8,128)(2,1)S(1)}, bf16[128,1024]{1,0:T(8,128)(2,1)S(1)}, u32[]{:S(2)}, u32[]{:S(2)}) collective-permute-start(bf16[128,1024]{1,0:T(8,128)(2,1)S(1)} %fusion.73), channel_id=1, source_target_pairs={{28,30},{29,31}} | collective-permute-start | bytes 786440 | tf_op jit(solution)/shard_map/ppermute | solution.py:23
  63.0 1.0 %copy-start.2 = (s32[1,16]{1,0:T(1,128)S(1)}, s32[1,16]{1,0:T(1,128)}, u32[]{:S(2)}) copy-start(s32[1,16]{1,0:T(1,128)} %param.11) | copy-start | bytes 196
  64.0 25.9 %copy-start = (bf16[256,2048]{1,0:T(8,128)(2,1)}, bf16[256,2048]{1,0:T(8,128)(2,1)S(1)}, u32[]{:S(2)}) copy-start(bf16[256,2048]{1,0:T(8,128)(2,1)S(1)} %fusion.118) | copy-start | bytes 3145732

commit v4 on v3

--- a/solution.py
+++ b/solution.py
@@ -30,6 +30,7 @@
     col_count = lax.axis_size("col")
     matrix = green[0, 0]
     half = matrix.shape[0] // 2
+    to_right, to_lower = lax.optimization_barrier((matrix[:, half:], matrix[:, :half]))
     stations = background.shape[2]
     own_source = (station_cell == row_place * col_count + col_place)[:, None]
     source = background[0, 0].astype(jnp.float32) + jnp.where(
@@ -53,14 +54,15 @@
             down_in, right_in = inbox.pop(moment)
             arrived = down_in + right_in
             rows_from = jnp.where(row_place == 0, half, 0)
-            rows = lax.dynamic_slice_in_dim(matrix, rows_from, half, 0)
-            right = (jnp.dot(arrived, rows[:, half:], preferred_element_type=jnp.float32) + part[:, half:]).astype(jnp.bfloat16)
-            lower = (jnp.dot(arrived, rows[:, :half], preferred_element_type=jnp.float32) + part[:, :half]).astype(jnp.bfloat16)
+            right_rows = lax.dynamic_slice_in_dim(to_right, rows_from, half, 0)
+            lower_rows = lax.dynamic_slice_in_dim(to_lower, rows_from, half, 0)
+            right = (jnp.dot(arrived, right_rows, preferred_element_type=jnp.float32) + part[:, half:]).astype(jnp.bfloat16)
+            lower = (jnp.dot(arrived, lower_rows, preferred_element_type=jnp.float32) + part[:, :half]).astype(jnp.bfloat16)
         else:
             down_in, right_in = inbox.pop(moment)
             joined = jnp.concatenate([down_in, right_in], axis=1)
-            right = (jnp.dot(joined, matrix[:, half:], preferred_element_type=jnp.float32) + part[:, half:]).astype(jnp.bfloat16)
-            lower = (jnp.dot(joined, matrix[:, :half], preferred_element_type=jnp.float32) + part[:, :half]).astype(jnp.bfloat16)
+            right = (jnp.dot(joined, to_right, preferred_element_type=jnp.float32) + part[:, half:]).astype(jnp.bfloat16)
+            lower = (jnp.dot(joined, to_lower, preferred_element_type=jnp.float32) + part[:, :half]).astype(jnp.bfloat16)
         right_next = passed_along(right, moment, False, row_count, col_count)
         down_next = passed_along(lower, moment, True, row_count, col_count)
         inbox[moment + SKEW] = (down_next, right_next)

time: 90.3 us -> 89.7 us (level)
  matrix products: 17.1 us -> 14.7 us
  local copies, waits for them, and re-layouts: 5.92 us -> 7.23 us
    slice x0 -> x1, local copies, waits for them, and re-layouts: none -> 5.93 us  [on_device(): matrix[:, :half]]
    dynamic_slice x1 -> x0, local copies, waits for them, and re-layouts: 4.73 us -> none  [on_device(): rows = lax.dynamic_slice_in_dim(matrix, rows_from, half, 0)]
    dot_general x14, matrix products: 15.8 us -> 13.4 us  [the longest x6 4.5 us: on_device(): jnp.dot(joined, to_lower, preferred_element_type=jnp.float32)]
  transfers between devices with their start and end apart: 14 -> 14, of which waited for: 3 -> 3; matrix products, arithmetic and copies ran while one was open for 14% -> 15% of each run, Pallas kernels for 0% -> 0%
where the time goes in v4:
time: 89.7 us; the launch traced here: 89.4 us
  blocking collectives  24.4 us (27%)
  waiting for transfers between devices  19.6 us (22%)
  starting transfers between devices  17.8 us (20%)
  matrix products  14.7 us (16%)
  local copies, waits for them, and re-layouts  7.23 us (8%)
  other arithmetic  4.52 us (5%)
  between operations  1.2 us (1%)
    all_to_all x1, blocking collectives, on_device(): lax.all_to_all(message, 'col', split_axis=0, concat_axis=0, tiled=True)  24.4 us
    ppermute x14, waiting for transfers between devices, passed_along(): return lax.ppermute(shard, ('row', 'col'), pairs)  19.6 us
    ppermute x14, starting transfers between devices, passed_along(): return lax.ppermute(shard, ('row', 'col'), pairs)  17.8 us
    slice x1, local copies, waits for them, and re-layouts, on_device(): matrix[:, :half]  5.93 us
    dot_general x6, matrix products, on_device(): jnp.dot(joined, to_lower, preferred_element_type=jnp.float32)  4.5 us
    dot_general x6, matrix products, on_device(): jnp.dot(joined, to_right, preferred_element_type=jnp.float32)  4.5 us
    dot_general x1, matrix products, on_device(): jnp.dot(arrived, lower_rows, preferred_element_type=jnp.float32)  2.27 us
    dot_general x1, matrix products, on_device(): jnp.dot(arrived, right_rows, preferred_element_type=jnp.float32)  2.15 us
  transfers between devices with their start and end apart: 14, of which 3 were waited for; matrix products, arithmetic and copies ran while one was open for 15% of the time, Pallas kernels for 0%

profile of v4, /device:TPU:24, one launch (start us, length us, event | category | flops | bytes accessed | tf_op | source)
XLA Modules:
  0.0 89.4 jit_solution(15228133945620796144)
XLA Ops:
  0.6 0.7 broadcast_compare_fusion
  1.3 1.9 %convert_add_fusion = f32[256,2048]{1,0:T(8,128)S(1)} fusion(bf16[256,2048]{1,0:T(8,128)(2,1)} %param.9, bf16[1,1,256,2048]{3,2,1,0:T(8,128)(2,1)} %param.8, pred[256]{0:T(512)(128)(4,1)S(1)} %broadcast_compare_fusion), kind=kLoop, calls=%fused_computation | loop fusion | flops 2097152 | bytes 4194560 | tf_op jit(solution)/shard_map/add | solution.py:36
  3.5 0.9 fusion.46
  5.0 1.4 %collective-permute-start.1 = (bf16[128,1024]{1,0:T(8,128)(2,1)}, bf16[128,1024]{1,0:T(8,128)(2,1)}, u32[]{:S(2)}, u32[]{:S(2)}) collective-permute-start(bf16[128,1024]{1,0:T(8,128)(2,1)} %get-tuple-element.10), channel_id=1, source_target_pairs={{0,2},{1,3}} | collective-permute-start | bytes 786440 | tf_op jit(solution)/shard_map/ppermute | solution.py:23
  6.4 5.9 %fusion.45 = (bf16[2048,1024]{1,0:T(8,128)(2,1)}, bf16[2048,1024]{1,0:T(8,128)(2,1)}) fusion(bf16[2048,2048]{1,0:T(8,128)(2,1)} %bitcast.41), kind=kLoop, calls=%fused_computation.85 | loop fusion | bytes 16777216 | tf_op jit(solution)/shard_map/slice | solution.py:33
  12.9 2.3 %fusion.13 = bf16[128,1024]{1,0:T(8,128)(2,1)S(1)} fusion(bf16[2048,1024]{1,0:T(8,128)(2,1)} %get-tuple-element.4, s32[]{:T(128)S(6)} %select_n.108, f32[256,2048]{1,0:T(8,128)S(1)} %convert_add_fusion, s32[]{:T(128)S(6)} %select_n.109, bf16[128,1024]{1,0:T(8,128)(2,1)S(1)} %collective-permute-done, bf16[128,1024]{1,0:T(8,128)(2,1)} %collective-permute-done.1), kind=kOutput, calls=%fused_computation.20 | convolution fusion | flops 268828672 | bytes 3407880 | tf_op jit(solution)/shard_map/dot_general | solution.py:60
  15.1 0.7 collective-permute-start.2
  15.8 2.1 %fusion.10 = bf16[128,1024]{1,0:T(8,128)(2,1)S(1)} fusion(bf16[2048,1024]{1,0:T(8,128)(2,1)} %get-tuple-element.5, s32[]{:T(128)S(6)} %select_n.108, f32[256,2048]{1,0:T(8,128)S(1)} %convert_add_fusion, s32[]{:T(128)S(6)} %select_n.109, s32[]{:T(128)S(6)} %add.147, bf16[128,1024]{1,0:T(8,128)(2,1)S(1)} %collective-permute-done, ...), kind=kOutput, calls=%fused_computation.19 | convolution fusion | flops 268828672 | bytes 3407884 | tf_op jit(solution)/shard_map/dot_general | solution.py:59
  18.0 0.8 collective-permute-start.3
  19.1 0.8 fusion.16
  19.8 1.3 %collective-permute-start.4 = (bf16[128,1024]{1,0:T(8,128)(2,1)S(1)}, bf16[128,1024]{1,0:T(8,128)(2,1)S(1)}, u32[]{:S(2)}, u32[]{:S(2)}) collective-permute-start(bf16[128,1024]{1,0:T(8,128)(2,1)S(1)} %fusion.16), channel_id=1, source_target_pairs={{2,10},{4,12},{8,16},{10,18},{16,24},{3,11},{5,13},{9,17},{11,19},... | collective-permute-start | bytes 786440 | tf_op jit(solution)/shard_map/ppermute | solution.py:23
  21.1 0.7 fusion.17
  21.9 0.7 collective-permute-start.5
  22.8 10.8 %collective-permute-done.4 = bf16[128,1024]{1,0:T(8,128)(2,1)S(1)} collective-permute-done((bf16[128,1024]{1,0:T(8,128)(2,1)S(1)}, bf16[128,1024]{1,0:T(8,128)(2,1)S(1)}, u32[]{:S(2)}, u32[]{:S(2)}) %collective-permute-start.4) | collective-permute-done | bytes 262176 | tf_op jit(solution)/shard_map/ppermute | solution.py:23
  33.6 0.8 fusion.18
  34.4 1.3 %collective-permute-start.6 = (bf16[128,1024]{1,0:T(8,128)(2,1)S(1)}, bf16[128,1024]{1,0:T(8,128)(2,1)S(1)}, u32[]{:S(2)}, u32[]{:S(2)}) collective-permute-start(bf16[128,1024]{1,0:T(8,128)(2,1)S(1)} %fusion.18), channel_id=1, source_target_pairs={{4,12},{6,14},{10,18},{12,20},{16,24},{18,26},{5,13},{7,15},{11,19... | collective-permute-start | bytes 786440 | tf_op jit(solution)/shard_map/ppermute | solution.py:23
  35.7 0.7 fusion.19
  36.4 1.3 %collective-permute-start.7 = (bf16[128,1024]{1,0:T(8,128)(2,1)S(1)}, bf16[128,1024]{1,0:T(8,128)(2,1)S(1)}, u32[]{:S(2)}, u32[]{:S(2)}) collective-permute-start(bf16[128,1024]{1,0:T(8,128)(2,1)S(1)} %fusion.19), channel_id=1, source_target_pairs={{4,6},{10,12},{12,14},{16,18},{18,20},{24,26},{5,7},{11,13},{13,15... | collective-permute-start | bytes 786440 | tf_op jit(solution)/shard_map/ppermute | solution.py:23
  37.9 5.1 %collective-permute-done.6 = bf16[128,1024]{1,0:T(8,128)(2,1)S(1)} collective-permute-done((bf16[128,1024]{1,0:T(8,128)(2,1)S(1)}, bf16[128,1024]{1,0:T(8,128)(2,1)S(1)}, u32[]{:S(2)}, u32[]{:S(2)}) %collective-permute-start.6) | collective-permute-done | bytes 262176 | tf_op jit(solution)/shard_map/ppermute | solution.py:23
  43.1 0.7 fusion.20
  43.9 0.7 collective-permute-start.8
  44.5 0.7 fusion.21
  45.3 6.3 %collective-permute-start.9 = (bf16[128,1024]{1,0:T(8,128)(2,1)S(1)}, bf16[128,1024]{1,0:T(8,128)(2,1)S(1)}, u32[]{:S(2)}, u32[]{:S(2)}) collective-permute-start(bf16[128,1024]{1,0:T(8,128)(2,1)S(1)} %fusion.21), channel_id=1, source_target_pairs={{12,14},{18,20},{20,22},{24,26},{26,28},{13,15},{19,21},{21,23},{2... | collective-permute-start | bytes 786440 | tf_op jit(solution)/shard_map/ppermute | solution.py:23
  51.8 3.6 %collective-permute-done.9 = bf16[128,1024]{1,0:T(8,128)(2,1)S(1)} collective-permute-done((bf16[128,1024]{1,0:T(8,128)(2,1)S(1)}, bf16[128,1024]{1,0:T(8,128)(2,1)S(1)}, u32[]{:S(2)}, u32[]{:S(2)}) %collective-permute-start.9) | collective-permute-done | bytes 262176 | tf_op jit(solution)/shard_map/ppermute | solution.py:23
  55.5 0.7 fusion.22
  56.9 0.7 fusion.23
  58.6 0.8 fusion.24
  60.0 0.7 fusion.25
  61.8 0.8 fusion.27
  62.5 0.7 fusion.26
  64.1 24.4 %all_to_all.5 = bf16[4,8,384]{2,1,0:T(8,128)(2,1)S(1)} all-to-all(bf16[4,8,384]{2,1,0:T(8,128)(2,1)S(1)} %maximum_bitcast_fusion), channel_id=1, replica_groups=mesh['row'=4,'col'=4,'batch'=2] {'col'}, dimensions={0} | all-to-all | bytes 49152 | tf_op jit(solution)/shard_map/all_to_all | solution.py:89
  88.5 0.8 convolution_bitcast_fusion
  (60 shorter events, 6.3 us)
Async XLA Ops:
  4.3 8.5 %collective-permute-start = (bf16[128,1024]{1,0:T(8,128)(2,1)}, bf16[128,1024]{1,0:T(8,128)(2,1)S(1)}, u32[]{:S(2)}, u32[]{:S(2)}) collective-permute-start(bf16[128,1024]{1,0:T(8,128)(2,1)} %get-tuple-element.11), channel_id=1, source_target_pairs={{0,8},{1,9}} | collective-permute-start | bytes 786440 | tf_op jit(solution)/shard_map/ppermute | solution.py:23
  5.0 7.8 %collective-permute-start.1 = (bf16[128,1024]{1,0:T(8,128)(2,1)}, bf16[128,1024]{1,0:T(8,128)(2,1)}, u32[]{:S(2)}, u32[]{:S(2)}) collective-permute-start(bf16[128,1024]{1,0:T(8,128)(2,1)} %get-tuple-element.10), channel_id=1, source_target_pairs={{0,2},{1,3}} | collective-permute-start | bytes 786440 | tf_op jit(solution)/shard_map/ppermute | solution.py:23
  6.4 5.9 %copy-start.5 = (s32[1,16]{1,0:T(1,128)S(1)}, s32[1,16]{1,0:T(1,128)}, u32[]{:S(2)}) copy-start(s32[1,16]{1,0:T(1,128)} %param.13) | copy-start | bytes 196
  6.4 5.9 %copy-start.3 = (s32[1,16,1]{1,2,0:T(1,128)S(1)}, s32[1,16,1]{1,2,0:T(1,128)}, u32[]{:S(2)}) copy-start(s32[1,16,1]{1,2,0:T(1,128)} %param.12) | copy-start | bytes 196
  12.8 6.2 %copy-start = (bf16[2048,1024]{1,0:T(8,128)(2,1)S(1)}, bf16[2048,1024]{1,0:T(8,128)(2,1)}, u32[]{:S(2)}) copy-start(bf16[2048,1024]{1,0:T(8,128)(2,1)} %get-tuple-element.4) | copy-start | bytes 12582916
  15.1 3.8 %collective-permute-start.2 = (bf16[128,1024]{1,0:T(8,128)(2,1)S(1)}, bf16[128,1024]{1,0:T(8,128)(2,1)S(1)}, u32[]{:S(2)}, u32[]{:S(2)}) collective-permute-start(bf16[128,1024]{1,0:T(8,128)(2,1)S(1)} %fusion.13), channel_id=1, source_target_pairs={{0,8},{2,10},{8,16},{1,9},{3,11},{9,17}} | collective-permute-start | bytes 786440 | tf_op jit(solution)/shard_map/ppermute | solution.py:23
  18.0 3.2 %copy-start.1 = (bf16[2048,1024]{1,0:T(8,128)(2,1)S(1)}, bf16[2048,1024]{1,0:T(8,128)(2,1)}, u32[]{:S(2)}) copy-start(bf16[2048,1024]{1,0:T(8,128)(2,1)} %get-tuple-element.5) | copy-start | bytes 12582916
  18.0 1.0 %collective-permute-start.3 = (bf16[128,1024]{1,0:T(8,128)(2,1)S(1)}, bf16[128,1024]{1,0:T(8,128)(2,1)S(1)}, u32[]{:S(2)}, u32[]{:S(2)}) collective-permute-start(bf16[128,1024]{1,0:T(8,128)(2,1)S(1)} %fusion.10), channel_id=1, source_target_pairs={{0,2},{2,4},{8,10},{1,3},{3,5},{9,11}} | collective-permute-start | bytes 786440 | tf_op jit(solution)/shard_map/ppermute | solution.py:23
  19.8 13.7 %collective-permute-start.4 = (bf16[128,1024]{1,0:T(8,128)(2,1)S(1)}, bf16[128,1024]{1,0:T(8,128)(2,1)S(1)}, u32[]{:S(2)}, u32[]{:S(2)}) collective-permute-start(bf16[128,1024]{1,0:T(8,128)(2,1)S(1)} %fusion.16), channel_id=1, source_target_pairs={{2,10},{4,12},{8,16},{10,18},{16,24},{3,11},{5,13},{9,17},{11,19},... | collective-permute-start | bytes 786440 | tf_op jit(solution)/shard_map/ppermute | solution.py:23
  21.9 11.7 %collective-permute-start.5 = (bf16[128,1024]{1,0:T(8,128)(2,1)S(1)}, bf16[128,1024]{1,0:T(8,128)(2,1)S(1)}, u32[]{:S(2)}, u32[]{:S(2)}) collective-permute-start(bf16[128,1024]{1,0:T(8,128)(2,1)S(1)} %fusion.17), channel_id=1, source_target_pairs={{2,4},{4,6},{8,10},{10,12},{16,18},{3,5},{5,7},{9,11},{11,13},{17,... | collective-permute-start | bytes 786440 | tf_op jit(solution)/shard_map/ppermute | solution.py:23
  34.4 8.7 %collective-permute-start.6 = (bf16[128,1024]{1,0:T(8,128)(2,1)S(1)}, bf16[128,1024]{1,0:T(8,128)(2,1)S(1)}, u32[]{:S(2)}, u32[]{:S(2)}) collective-permute-start(bf16[128,1024]{1,0:T(8,128)(2,1)S(1)} %fusion.18), channel_id=1, source_target_pairs={{4,12},{6,14},{10,18},{12,20},{16,24},{18,26},{5,13},{7,15},{11,19... | collective-permute-start | bytes 786440 | tf_op jit(solution)/shard_map/ppermute | solution.py:23
  36.4 6.7 %collective-permute-start.7 = (bf16[128,1024]{1,0:T(8,128)(2,1)S(1)}, bf16[128,1024]{1,0:T(8,128)(2,1)S(1)}, u32[]{:S(2)}, u32[]{:S(2)}) collective-permute-start(bf16[128,1024]{1,0:T(8,128)(2,1)S(1)} %fusion.19), channel_id=1, source_target_pairs={{4,6},{10,12},{12,14},{16,18},{18,20},{24,26},{5,7},{11,13},{13,15... | collective-permute-start | bytes 786440 | tf_op jit(solution)/shard_map/ppermute | solution.py:23
  43.9 7.9 %collective-permute-start.8 = (bf16[128,1024]{1,0:T(8,128)(2,1)S(1)}, bf16[128,1024]{1,0:T(8,128)(2,1)S(1)}, u32[]{:S(2)}, u32[]{:S(2)}) collective-permute-start(bf16[128,1024]{1,0:T(8,128)(2,1)S(1)} %fusion.20), channel_id=1, source_target_pairs={{6,14},{12,20},{14,22},{18,26},{20,28},{7,15},{13,21},{15,23},{19,... | collective-permute-start | bytes 786440 | tf_op jit(solution)/shard_map/ppermute | solution.py:23
  45.3 10.1 %collective-permute-start.9 = (bf16[128,1024]{1,0:T(8,128)(2,1)S(1)}, bf16[128,1024]{1,0:T(8,128)(2,1)S(1)}, u32[]{:S(2)}, u32[]{:S(2)}) collective-permute-start(bf16[128,1024]{1,0:T(8,128)(2,1)S(1)} %fusion.21), channel_id=1, source_target_pairs={{12,14},{18,20},{20,22},{24,26},{26,28},{13,15},{19,21},{21,23},{2... | collective-permute-start | bytes 786440 | tf_op jit(solution)/shard_map/ppermute | solution.py:23
  56.2 2.3 %collective-permute-start.10 = (bf16[128,1024]{1,0:T(8,128)(2,1)S(1)}, bf16[128,1024]{1,0:T(8,128)(2,1)S(1)}, u32[]{:S(2)}, u32[]{:S(2)}) collective-permute-start(bf16[128,1024]{1,0:T(8,128)(2,1)S(1)} %fusion.22), channel_id=1, source_target_pairs={{14,22},{20,28},{22,30},{15,23},{21,29},{23,31}} | collective-permute-start | bytes 786440 | tf_op jit(solution)/shard_map/ppermute | solution.py:23
  57.7 0.9 %collective-permute-start.11 = (bf16[128,1024]{1,0:T(8,128)(2,1)S(1)}, bf16[128,1024]{1,0:T(8,128)(2,1)S(1)}, u32[]{:S(2)}, u32[]{:S(2)}) collective-permute-start(bf16[128,1024]{1,0:T(8,128)(2,1)S(1)} %fusion.23), channel_id=1, source_target_pairs={{20,22},{26,28},{28,30},{21,23},{27,29},{29,31}} | collective-permute-start | bytes 786440 | tf_op jit(solution)/shard_map/ppermute | solution.py:23
  59.4 2.3 %collective-permute-start.12 = (bf16[128,1024]{1,0:T(8,128)(2,1)S(1)}, bf16[128,1024]{1,0:T(8,128)(2,1)S(1)}, u32[]{:S(2)}, u32[]{:S(2)}) collective-permute-start(bf16[128,1024]{1,0:T(8,128)(2,1)S(1)} %fusion.24), channel_id=1, source_target_pairs={{22,30},{23,31}} | collective-permute-start | bytes 786440 | tf_op jit(solution)/shard_map/ppermute | solution.py:23
  60.8 0.9 %collective-permute-start.13 = (bf16[128,1024]{1,0:T(8,128)(2,1)S(1)}, bf16[128,1024]{1,0:T(8,128)(2,1)S(1)}, u32[]{:S(2)}, u32[]{:S(2)}) collective-permute-start(bf16[128,1024]{1,0:T(8,128)(2,1)S(1)} %fusion.25), channel_id=1, source_target_pairs={{28,30},{29,31}} | collective-permute-start | bytes 786440 | tf_op jit(solution)/shard_map/ppermute | solution.py:23
  62.5 1.0 %copy-start.4 = (s32[1,16]{1,0:T(1,128)S(1)}, s32[1,16]{1,0:T(1,128)}, u32[]{:S(2)}) copy-start(s32[1,16]{1,0:T(1,128)} %param.11) | copy-start | bytes 196
  63.5 25.9 %copy-start.2 = (bf16[256,2048]{1,0:T(8,128)(2,1)}, bf16[256,2048]{1,0:T(8,128)(2,1)S(1)}, u32[]{:S(2)}) copy-start(bf16[256,2048]{1,0:T(8,128)(2,1)S(1)} %fusion.34) | copy-start | bytes 3145732

commit v5 on v4

--- a/solution.py
+++ b/solution.py
@@ -48,8 +48,11 @@
         start = jnp.clip(block, 0, BLOCKS - 1) * height
         part = lax.dynamic_slice_in_dim(source, start, height, 0)
         if moment < SKEW:
-            lower = part[:, :half].astype(jnp.bfloat16)
-            right = part[:, half:].astype(jnp.bfloat16)
+            first = background[0, 0, :height].astype(jnp.float32) + jnp.where(
+                own_source[:height], wavelet[:height].astype(jnp.float32), 0.0
+            )
+            lower = first[:, :half].astype(jnp.bfloat16)
+            right = first[:, half:].astype(jnp.bfloat16)
         elif moment == SKEW and SKEW == 1:
             down_in, right_in = inbox.pop(moment)
             arrived = down_in + right_in

time: 89.7 us -> 89 us (level)
  local copies, waits for them, and re-layouts: 7.23 us -> 5.01 us
  other arithmetic: 4.52 us -> 6.06 us
    slice x1, local copies, waits for them, and re-layouts: 5.93 us -> 3.71 us  [on_device(): matrix[:, :half]]
    dynamic_update_slice x8, other arithmetic: 1.44 us -> 2.97 us  [on_device(): lax.dynamic_update_slice_in_dim(field, jnp.where(active, update, previous...]
where the time goes in v5:
time: 89 us; the launch traced here: 88.6 us
  blocking collectives  24.4 us (27%)
  waiting for transfers between devices  19.3 us (22%)
  starting transfers between devices  17.9 us (20%)
  matrix products  14.7 us (17%)
  other arithmetic  6.06 us (7%)
  local copies, waits for them, and re-layouts  5.01 us (6%)
  between operations  1.22 us (1%)
    all_to_all x1, blocking collectives, on_device(): lax.all_to_all(message, 'col', split_axis=0, concat_axis=0, tiled=True)  24.4 us
    ppermute x14, waiting for transfers between devices, passed_along(): return lax.ppermute(shard, ('row', 'col'), pairs)  19.3 us
    ppermute x14, starting transfers between devices, passed_along(): return lax.ppermute(shard, ('row', 'col'), pairs)  17.9 us
    dot_general x6, matrix products, on_device(): jnp.dot(joined, to_lower, preferred_element_type=jnp.float32)  4.5 us
    dot_general x6, matrix products, on_device(): jnp.dot(joined, to_right, preferred_element_type=jnp.float32)  4.5 us
    slice x1, local copies, waits for them, and re-layouts, on_device(): matrix[:, :half]  3.71 us
    dynamic_update_slice x8, other arithmetic, on_device(): lax.dynamic_update_slice_in_dim(field, jnp.where(active, update, previous...  2.97 us
    dot_general x1, matrix products, on_device(): jnp.dot(arrived, lower_rows, preferred_element_type=jnp.float32)  2.28 us
  transfers between devices with their start and end apart: 14, of which 3 were waited for; matrix products, arithmetic and copies ran while one was open for 15% of the time, Pallas kernels for 0%

profile of v5, /device:TPU:24, one launch (start us, length us, event | category | flops | bytes accessed | tf_op | source)
XLA Modules:
  0.0 88.6 jit_solution(18013284270760817085)
XLA Ops:
  0.6 0.7 broadcast_compare_fusion
  1.4 1.7 %select_dynamic-update-slice_fusion = (bf16[256,2048]{1,0:T(8,128)(2,1)S(1)}, bf16[128,2048]{1,0:T(8,128)(2,1)S(1)}) fusion(bf16[256,2048]{1,0:T(8,128)(2,1)S(1)} %broadcast_in_dim.60, s32[]{:T(128)S(6)} %select_n.109, pred[]{:T(512)S(6)} %and.26, bf16[256,2048]{1,0:T(8,128)(2,1)} %param.9, pred[128]{0:T(512)(128)(4,1)S(1)} %bitcast.49, ...), kind=kLoop, calls=%fused_computation.52 | loop fusion | flops 1572864 | bytes 2097669 | tf_op jit(solution)/shard_map/dynamic_update_slice | solution.py:74
  3.1 0.9 fusion.48
  4.0 0.8 collective-permute-start
  4.8 1.4 %collective-permute-start.1 = (bf16[128,1024]{1,0:T(8,128)(2,1)}, bf16[128,1024]{1,0:T(8,128)(2,1)}, u32[]{:S(2)}, u32[]{:S(2)}) collective-permute-start(bf16[128,1024]{1,0:T(8,128)(2,1)} %get-tuple-element.10), channel_id=1, source_target_pairs={{0,2},{1,3}} | collective-permute-start | bytes 786440 | tf_op jit(solution)/shard_map/ppermute | solution.py:23
  6.2 1.9 %convert_add_fusion = f32[256,2048]{1,0:T(8,128)S(1)} fusion(bf16[256,2048]{1,0:T(8,128)(2,1)} %param.9, bf16[1,1,256,2048]{3,2,1,0:T(8,128)(2,1)} %param.8, pred[256]{0:T(512)(128)(4,1)S(1)} %broadcast_compare_fusion), kind=kLoop, calls=%fused_computation | loop fusion | flops 2097152 | bytes 4194560 | tf_op jit(solution)/shard_map/add | solution.py:36
  8.1 3.7 %fusion.47 = (bf16[2048,1024]{1,0:T(8,128)(2,1)}, bf16[2048,1024]{1,0:T(8,128)(2,1)}) fusion(bf16[2048,2048]{1,0:T(8,128)(2,1)S(1)} %bitcast.46), kind=kLoop, calls=%fused_computation.86 | loop fusion | bytes 16777216 | tf_op jit(solution)/shard_map/slice | solution.py:33
  12.3 2.3 %fusion.13 = bf16[128,1024]{1,0:T(8,128)(2,1)S(1)} fusion(bf16[2048,1024]{1,0:T(8,128)(2,1)} %get-tuple-element.4, s32[]{:T(128)S(6)} %select_n.111, f32[256,2048]{1,0:T(8,128)S(1)} %convert_add_fusion, s32[]{:T(128)S(6)} %select_n.113, bf16[128,1024]{1,0:T(8,128)(2,1)S(1)} %collective-permute-done, bf16[128,1024]{1,0:T(8,128)(2,1)} %collective-permute-done.1), kind=kOutput, calls=%fused_computation.20 | convolution fusion | flops 268828672 | bytes 3407880 | tf_op jit(solution)/shard_map/dot_general | solution.py:63
  15.3 2.1 %fusion.10 = bf16[128,1024]{1,0:T(8,128)(2,1)S(1)} fusion(bf16[2048,1024]{1,0:T(8,128)(2,1)} %get-tuple-element.5, s32[]{:T(128)S(6)} %select_n.111, f32[256,2048]{1,0:T(8,128)S(1)} %convert_add_fusion, s32[]{:T(128)S(6)} %select_n.113, s32[]{:T(128)S(6)} %add.150, bf16[128,1024]{1,0:T(8,128)(2,1)S(1)} %collective-permute-done, ...), kind=kOutput, calls=%fused_computation.19 | convolution fusion | flops 268828672 | bytes 3407884 | tf_op jit(solution)/shard_map/dot_general | solution.py:62
  17.5 0.8 collective-permute-start.3
  18.6 0.7 fusion.16
  19.3 1.3 %collective-permute-start.4 = (bf16[128,1024]{1,0:T(8,128)(2,1)S(1)}, bf16[128,1024]{1,0:T(8,128)(2,1)S(1)}, u32[]{:S(2)}, u32[]{:S(2)}) collective-permute-start(bf16[128,1024]{1,0:T(8,128)(2,1)S(1)} %fusion.16), channel_id=1, source_target_pairs={{2,10},{4,12},{8,16},{10,18},{16,24},{3,11},{5,13},{9,17},{11,19},... | collective-permute-start | bytes 786440 | tf_op jit(solution)/shard_map/ppermute | solution.py:23
  20.6 0.7 fusion.17
  21.4 0.7 collective-permute-start.5
  22.2 10.7 %collective-permute-done.4 = bf16[128,1024]{1,0:T(8,128)(2,1)S(1)} collective-permute-done((bf16[128,1024]{1,0:T(8,128)(2,1)S(1)}, bf16[128,1024]{1,0:T(8,128)(2,1)S(1)}, u32[]{:S(2)}, u32[]{:S(2)}) %collective-permute-start.4) | collective-permute-done | bytes 262176 | tf_op jit(solution)/shard_map/ppermute | solution.py:23
  33.0 0.8 fusion.18
  33.7 1.3 %collective-permute-start.6 = (bf16[128,1024]{1,0:T(8,128)(2,1)S(1)}, bf16[128,1024]{1,0:T(8,128)(2,1)S(1)}, u32[]{:S(2)}, u32[]{:S(2)}) collective-permute-start(bf16[128,1024]{1,0:T(8,128)(2,1)S(1)} %fusion.18), channel_id=1, source_target_pairs={{4,12},{6,14},{10,18},{12,20},{16,24},{18,26},{5,13},{7,15},{11,19... | collective-permute-start | bytes 786440 | tf_op jit(solution)/shard_map/ppermute | solution.py:23
  35.0 0.7 fusion.19
  35.8 1.3 %collective-permute-start.7 = (bf16[128,1024]{1,0:T(8,128)(2,1)S(1)}, bf16[128,1024]{1,0:T(8,128)(2,1)S(1)}, u32[]{:S(2)}, u32[]{:S(2)}) collective-permute-start(bf16[128,1024]{1,0:T(8,128)(2,1)S(1)} %fusion.19), channel_id=1, source_target_pairs={{4,6},{10,12},{12,14},{16,18},{18,20},{24,26},{5,7},{11,13},{13,15... | collective-permute-start | bytes 786440 | tf_op jit(solution)/shard_map/ppermute | solution.py:23
  37.3 5.0 %collective-permute-done.6 = bf16[128,1024]{1,0:T(8,128)(2,1)S(1)} collective-permute-done((bf16[128,1024]{1,0:T(8,128)(2,1)S(1)}, bf16[128,1024]{1,0:T(8,128)(2,1)S(1)}, u32[]{:S(2)}, u32[]{:S(2)}) %collective-permute-start.6) | collective-permute-done | bytes 262176 | tf_op jit(solution)/shard_map/ppermute | solution.py:23
  42.4 0.7 fusion.20
  43.8 0.7 fusion.21
  44.6 6.3 %collective-permute-start.9 = (bf16[128,1024]{1,0:T(8,128)(2,1)S(1)}, bf16[128,1024]{1,0:T(8,128)(2,1)S(1)}, u32[]{:S(2)}, u32[]{:S(2)}) collective-permute-start(bf16[128,1024]{1,0:T(8,128)(2,1)S(1)} %fusion.21), channel_id=1, source_target_pairs={{12,14},{18,20},{20,22},{24,26},{26,28},{13,15},{19,21},{21,23},{2... | collective-permute-start | bytes 786440 | tf_op jit(solution)/shard_map/ppermute | solution.py:23
  51.1 3.6 %collective-permute-done.9 = bf16[128,1024]{1,0:T(8,128)(2,1)S(1)} collective-permute-done((bf16[128,1024]{1,0:T(8,128)(2,1)S(1)}, bf16[128,1024]{1,0:T(8,128)(2,1)S(1)}, u32[]{:S(2)}, u32[]{:S(2)}) %collective-permute-start.9) | collective-permute-done | bytes 262176 | tf_op jit(solution)/shard_map/ppermute | solution.py:23
  54.7 0.7 fusion.22
  56.2 0.7 fusion.23
  57.9 0.7 fusion.24
  59.3 0.7 fusion.25
  61.0 0.8 fusion.27
  61.8 0.8 fusion.26
  63.3 24.4 %all_to_all.5 = bf16[4,8,384]{2,1,0:T(8,128)(2,1)S(1)} all-to-all(bf16[4,8,384]{2,1,0:T(8,128)(2,1)S(1)} %maximum_bitcast_fusion), channel_id=1, replica_groups=mesh['row'=4,'col'=4,'batch'=2] {'col'}, dimensions={0} | all-to-all | bytes 49152 | tf_op jit(solution)/shard_map/all_to_all | solution.py:92
  87.8 0.8 convolution_bitcast_fusion
  (62 shorter events, 6.8 us)
Async XLA Ops:
  1.3 6.8 %copy-start.3 = (bf16[1,1,2048,2048]{3,2,1,0:T(8,128)(2,1)S(1)}, bf16[1,1,2048,2048]{3,2,1,0:T(8,128)(2,1)}, u32[]{:S(2)}) copy-start(bf16[1,1,2048,2048]{3,2,1,0:T(8,128)(2,1)} %param.7) | copy-start | bytes 25165828
  4.0 8.3 %collective-permute-start = (bf16[128,1024]{1,0:T(8,128)(2,1)}, bf16[128,1024]{1,0:T(8,128)(2,1)S(1)}, u32[]{:S(2)}, u32[]{:S(2)}) collective-permute-start(bf16[128,1024]{1,0:T(8,128)(2,1)} %get-tuple-element.11), channel_id=1, source_target_pairs={{0,8},{1,9}} | collective-permute-start | bytes 786440 | tf_op jit(solution)/shard_map/ppermute | solution.py:23
  4.8 7.5 %collective-permute-start.1 = (bf16[128,1024]{1,0:T(8,128)(2,1)}, bf16[128,1024]{1,0:T(8,128)(2,1)}, u32[]{:S(2)}, u32[]{:S(2)}) collective-permute-start(bf16[128,1024]{1,0:T(8,128)(2,1)} %get-tuple-element.10), channel_id=1, source_target_pairs={{0,2},{1,3}} | collective-permute-start | bytes 786440 | tf_op jit(solution)/shard_map/ppermute | solution.py:23
  8.1 3.7 %copy-start.6 = (s32[1,16]{1,0:T(1,128)S(1)}, s32[1,16]{1,0:T(1,128)}, u32[]{:S(2)}) copy-start(s32[1,16]{1,0:T(1,128)} %param.13) | copy-start | bytes 196
  8.1 3.7 %copy-start.4 = (s32[1,16,1]{1,2,0:T(1,128)S(1)}, s32[1,16,1]{1,2,0:T(1,128)}, u32[]{:S(2)}) copy-start(s32[1,16,1]{1,2,0:T(1,128)} %param.12) | copy-start | bytes 196
  12.3 6.2 %copy-start = (bf16[2048,1024]{1,0:T(8,128)(2,1)S(1)}, bf16[2048,1024]{1,0:T(8,128)(2,1)}, u32[]{:S(2)}) copy-start(bf16[2048,1024]{1,0:T(8,128)(2,1)} %get-tuple-element.4) | copy-start | bytes 12582916
  14.6 3.8 %collective-permute-start.2 = (bf16[128,1024]{1,0:T(8,128)(2,1)S(1)}, bf16[128,1024]{1,0:T(8,128)(2,1)S(1)}, u32[]{:S(2)}, u32[]{:S(2)}) collective-permute-start(bf16[128,1024]{1,0:T(8,128)(2,1)S(1)} %fusion.13), channel_id=1, source_target_pairs={{0,8},{2,10},{8,16},{1,9},{3,11},{9,17}} | collective-permute-start | bytes 786440 | tf_op jit(solution)/shard_map/ppermute | solution.py:23
  17.5 3.1 %copy-start.1 = (bf16[2048,1024]{1,0:T(8,128)(2,1)S(1)}, bf16[2048,1024]{1,0:T(8,128)(2,1)}, u32[]{:S(2)}) copy-start(bf16[2048,1024]{1,0:T(8,128)(2,1)} %get-tuple-element.5) | copy-start | bytes 12582916
  17.5 1.0 %collective-permute-start.3 = (bf16[128,1024]{1,0:T(8,128)(2,1)S(1)}, bf16[128,1024]{1,0:T(8,128)(2,1)S(1)}, u32[]{:S(2)}, u32[]{:S(2)}) collective-permute-start(bf16[128,1024]{1,0:T(8,128)(2,1)S(1)} %fusion.10), channel_id=1, source_target_pairs={{0,2},{2,4},{8,10},{1,3},{3,5},{9,11}} | collective-permute-start | bytes 786440 | tf_op jit(solution)/shard_map/ppermute | solution.py:23
  19.3 13.6 %collective-permute-start.4 = (bf16[128,1024]{1,0:T(8,128)(2,1)S(1)}, bf16[128,1024]{1,0:T(8,128)(2,1)S(1)}, u32[]{:S(2)}, u32[]{:S(2)}) collective-permute-start(bf16[128,1024]{1,0:T(8,128)(2,1)S(1)} %fusion.16), channel_id=1, source_target_pairs={{2,10},{4,12},{8,16},{10,18},{16,24},{3,11},{5,13},{9,17},{11,19},... | collective-permute-start | bytes 786440 | tf_op jit(solution)/shard_map/ppermute | solution.py:23
  21.4 11.6 %collective-permute-start.5 = (bf16[128,1024]{1,0:T(8,128)(2,1)S(1)}, bf16[128,1024]{1,0:T(8,128)(2,1)S(1)}, u32[]{:S(2)}, u32[]{:S(2)}) collective-permute-start(bf16[128,1024]{1,0:T(8,128)(2,1)S(1)} %fusion.17), channel_id=1, source_target_pairs={{2,4},{4,6},{8,10},{10,12},{16,18},{3,5},{5,7},{9,11},{11,13},{17,... | collective-permute-start | bytes 786440 | tf_op jit(solution)/shard_map/ppermute | solution.py:23
  33.7 8.6 %collective-permute-start.6 = (bf16[128,1024]{1,0:T(8,128)(2,1)S(1)}, bf16[128,1024]{1,0:T(8,128)(2,1)S(1)}, u32[]{:S(2)}, u32[]{:S(2)}) collective-permute-start(bf16[128,1024]{1,0:T(8,128)(2,1)S(1)} %fusion.18), channel_id=1, source_target_pairs={{4,12},{6,14},{10,18},{12,20},{16,24},{18,26},{5,13},{7,15},{11,19... | collective-permute-start | bytes 786440 | tf_op jit(solution)/shard_map/ppermute | solution.py:23
  35.8 6.5 %collective-permute-start.7 = (bf16[128,1024]{1,0:T(8,128)(2,1)S(1)}, bf16[128,1024]{1,0:T(8,128)(2,1)S(1)}, u32[]{:S(2)}, u32[]{:S(2)}) collective-permute-start(bf16[128,1024]{1,0:T(8,128)(2,1)S(1)} %fusion.19), channel_id=1, source_target_pairs={{4,6},{10,12},{12,14},{16,18},{18,20},{24,26},{5,7},{11,13},{13,15... | collective-permute-start | bytes 786440 | tf_op jit(solution)/shard_map/ppermute | solution.py:23
  43.1 7.9 %collective-permute-start.8 = (bf16[128,1024]{1,0:T(8,128)(2,1)S(1)}, bf16[128,1024]{1,0:T(8,128)(2,1)S(1)}, u32[]{:S(2)}, u32[]{:S(2)}) collective-permute-start(bf16[128,1024]{1,0:T(8,128)(2,1)S(1)} %fusion.20), channel_id=1, source_target_pairs={{6,14},{12,20},{14,22},{18,26},{20,28},{7,15},{13,21},{15,23},{19,... | collective-permute-start | bytes 786440 | tf_op jit(solution)/shard_map/ppermute | solution.py:23
  44.6 10.1 %collective-permute-start.9 = (bf16[128,1024]{1,0:T(8,128)(2,1)S(1)}, bf16[128,1024]{1,0:T(8,128)(2,1)S(1)}, u32[]{:S(2)}, u32[]{:S(2)}) collective-permute-start(bf16[128,1024]{1,0:T(8,128)(2,1)S(1)} %fusion.21), channel_id=1, source_target_pairs={{12,14},{18,20},{20,22},{24,26},{26,28},{13,15},{19,21},{21,23},{2... | collective-permute-start | bytes 786440 | tf_op jit(solution)/shard_map/ppermute | solution.py:23
  55.5 2.3 %collective-permute-start.10 = (bf16[128,1024]{1,0:T(8,128)(2,1)S(1)}, bf16[128,1024]{1,0:T(8,128)(2,1)S(1)}, u32[]{:S(2)}, u32[]{:S(2)}) collective-permute-start(bf16[128,1024]{1,0:T(8,128)(2,1)S(1)} %fusion.22), channel_id=1, source_target_pairs={{14,22},{20,28},{22,30},{15,23},{21,29},{23,31}} | collective-permute-start | bytes 786440 | tf_op jit(solution)/shard_map/ppermute | solution.py:23
  56.9 0.9 %collective-permute-start.11 = (bf16[128,1024]{1,0:T(8,128)(2,1)S(1)}, bf16[128,1024]{1,0:T(8,128)(2,1)S(1)}, u32[]{:S(2)}, u32[]{:S(2)}) collective-permute-start(bf16[128,1024]{1,0:T(8,128)(2,1)S(1)} %fusion.23), channel_id=1, source_target_pairs={{20,22},{26,28},{28,30},{21,23},{27,29},{29,31}} | collective-permute-start | bytes 786440 | tf_op jit(solution)/shard_map/ppermute | solution.py:23
  58.6 2.3 %collective-permute-start.12 = (bf16[128,1024]{1,0:T(8,128)(2,1)S(1)}, bf16[128,1024]{1,0:T(8,128)(2,1)S(1)}, u32[]{:S(2)}, u32[]{:S(2)}) collective-permute-start(bf16[128,1024]{1,0:T(8,128)(2,1)S(1)} %fusion.24), channel_id=1, source_target_pairs={{22,30},{23,31}} | collective-permute-start | bytes 786440 | tf_op jit(solution)/shard_map/ppermute | solution.py:23
  60.1 0.9 %collective-permute-start.13 = (bf16[128,1024]{1,0:T(8,128)(2,1)S(1)}, bf16[128,1024]{1,0:T(8,128)(2,1)S(1)}, u32[]{:S(2)}, u32[]{:S(2)}) collective-permute-start(bf16[128,1024]{1,0:T(8,128)(2,1)S(1)} %fusion.25), channel_id=1, source_target_pairs={{28,30},{29,31}} | collective-permute-start | bytes 786440 | tf_op jit(solution)/shard_map/ppermute | solution.py:23
  61.8 1.0 %copy-start.5 = (s32[1,16]{1,0:T(1,128)S(1)}, s32[1,16]{1,0:T(1,128)}, u32[]{:S(2)}) copy-start(s32[1,16]{1,0:T(1,128)} %param.11) | copy-start | bytes 196
  62.7 25.9 %copy-start.2 = (bf16[256,2048]{1,0:T(8,128)(2,1)}, bf16[256,2048]{1,0:T(8,128)(2,1)S(1)}, u32[]{:S(2)}) copy-start(bf16[256,2048]{1,0:T(8,128)(2,1)S(1)} %fusion.35) | copy-start | bytes 3145732
